TPU v7x, 256 devices: a whole 4x4x8 slice. The times are simulated.
256 devices in a mesh: dp: 16 (over z, core), group: 16 (over x, y).
Axes of the slice: x: 4, y: 4, z: 8, core: 2. Of those that a mesh axis runs over, the one named last changes fastest.
Arguments:
- hidden_in: bfloat16 [16, 16, 128, 5120], P('dp', 'group'), may hold values from -48 to 48
- gain: float32 [5120], replicated, may hold values from 0.1 to 1.9
- value_weight: bfloat16 [5120, 512], P(('dp', 'group')), may hold values from -0.078125 to 0.078125
- value_cot: bfloat16 [16, 16, 128, 512], P('dp', 'group'), may hold values from -6 to 6
- lengths: int32 [16, 16], P('dp', 'group'), may hold values from 1 to 128, as said below
- rewards: int32 [16, 16], P('dp', 'group'), may hold values from 0 to 3
Outputs:
- values: bfloat16 [16, 16, 128, 512], P('dp', 'group')
- weight_grad: float32 [5120, 512], P(('dp', 'group'))
- gain_grad: float32 [5120], P(('dp', 'group'))
Inputs may be any that keep to these rules, and one draw needn't show every extreme that they name: `lengths`: some response has exactly 128 tokens.
All inputs are finite; a program needn't handle non-finite values.
Results may differ from a plain program's by a relative error of at most 0.019.
Values may be sent and summed in bfloat16 or wider, within the bound.
No kernel may reach another device: no remote copies, remote signals or barrier semaphores. Data moves between devices by JAX's collectives and lax.ppermute only.
A program may use at most 64 MiB of HBM per device.

v0:
```python
import jax
import jax.numpy as jnp
from jax import lax
from jax.sharding import PartitionSpec as P


def body(hidden_in, gain, value_weight, value_cot, lengths, rewards):
    prompts, answers, length, features = hidden_in.shape
    kv_width = value_weight.shape[1]
    row_count = prompts * answers * length
    group_count = answers * lax.axis_size("group")
    scores = rewards.astype(jnp.float32)
    reward_sum, square_sum = lax.psum(
        (jnp.sum(scores, axis=1, keepdims=True), jnp.sum(scores * scores, axis=1, keepdims=True)),
        "group",
    )
    centre = reward_sum / group_count
    spread = square_sum / group_count - centre * centre
    advantage = (scores - centre) / jnp.maximum(jnp.sqrt(spread), 1.0)
    position = jnp.arange(length)
    alive_mask = position[None, None, :] < lengths[:, :, None]
    token_weight = jnp.where(alive_mask, (advantage / lengths.astype(jnp.float32))[:, :, None], 0.0)
    flat_in = hidden_in.reshape(row_count, features)
    inverse = lax.rsqrt(
        jnp.mean(jnp.square(flat_in.astype(jnp.float32)), axis=1, keepdims=True) + 1e-06
    )
    normed = (flat_in.astype(jnp.float32) * inverse * gain).astype(jnp.bfloat16)
    scaled_cot = (
        token_weight.reshape(row_count, 1)
        * value_cot.reshape(row_count, kv_width).astype(jnp.float32)
    ).astype(jnp.bfloat16)
    full_weight = lax.all_gather(value_weight, ("dp", "group"), axis=0, tiled=True)
    projected = jnp.dot(normed, full_weight, preferred_element_type=jnp.float32)
    back = lax.dot_general(
        scaled_cot, full_weight, (((1,), (1,)), ((), ())), preferred_element_type=jnp.float32
    )
    gain_term = jnp.sum(back * (flat_in.astype(jnp.float32) * inverse), axis=0)
    values = projected.astype(jnp.bfloat16).reshape(prompts, answers, length, kv_width)
    gain_grad = lax.psum_scatter(gain_term, ("dp", "group"), scatter_dimension=0, tiled=True)
    weight_grad = lax.psum_scatter(
        lax.dot_general(
            normed, scaled_cot, (((0,), (0,)), ((), ())), preferred_element_type=jnp.float32
        ),
        ("dp", "group"),
        scatter_dimension=0,
        tiled=True,
    )
    return (values, weight_grad, gain_grad)


def solution(mesh):
    in_specs = (
        P("dp", "group", None, None),
        P(),
        P(("dp", "group"), None),
        P("dp", "group", None, None),
        P("dp", "group"),
        P("dp", "group"),
    )
    out_specs = (P("dp", "group", None, None), P(("dp", "group"), None), P(("dp", "group")))
    return jax.shard_map(body, mesh=mesh, in_specs=in_specs, out_specs=out_specs, check_vma=False)
```

profile of v0, /device:TPU:97, one launch (start us, length us, event | category | flops | bytes accessed | tf_op | source)
XLA Modules:
  0.0 1105.8 jit_solution(11816118906791334442)
XLA Ops:
  8.5 33.9 %all-reduce.3 = (f32[1,1]{1,0:T(1,128)}, f32[1,1]{1,0:T(1,128)}) all-reduce(f32[1,1]{1,0:T(1,128)S(6)} %convert_element_type.52, f32[1,1]{1,0:T(1,128)S(6)} %mul.62), channel_id=1, replica_groups=mesh['dp'=16,'group'=16] {'group'}, use_global_device_ids=true, to_apply=%region_1.0 | all-reduce | flops 2 | bytes 16 | tf_op jit(solution)/shard_map/psum | solution.py:13
  48.1 7.0 fusion.10
  55.1 676.3 %fusion = f32[24,512]{1,0:T(8,128)S(1)} fusion(f32[5120,512]{1,0:T(8,128)} %fusion.10), kind=kCustom, calls=%all-reduce-scatter | all-reduce-scatter fusion | flops 3145729 | bytes 10534912
  731.4 1.9 collective-permute-start.41
  733.3 1.9 collective-permute-start.40
  735.3 8.6 collective-permute-start.42
  743.9 1.9 collective-permute-start.39
  745.9 1.9 collective-permute-start.38
  747.8 4.1 collective-permute-start.37
  751.9 10.8 collective-permute-start.36
  762.7 4.6 collective-permute-start.35
  767.3 8.0 collective-permute-start.34
  775.4 26.1 %collective-permute-start.33 = (f32[24,512]{1,0:T(8,128)S(1)}, f32[24,512]{1,0:T(8,128)S(1)}, u32[]{:S(2)}, u32[]{:S(2)}) collective-permute-start(f32[24,512]{1,0:T(8,128)S(1)} %fusion), channel_id=1, source_target_pairs={{0,34},{1,35},{2,36},{3,37},{4,38},{5,39},{6,40},{7,41},{8,42},{9,... | collective-permute-start | bytes 147464
  801.6 2.0 collective-permute-start.32
  803.6 2.5 collective-permute-start.31
  806.1 5.8 collective-permute-start.30
  812.0 1.9 collective-permute-start.29
  813.9 1.9 collective-permute-start.28
  815.8 1.9 collective-permute-start.27
  817.8 2.8 collective-permute-start.26
  820.6 1.9 collective-permute-start.25
  822.5 2.1 collective-permute-start.24
  824.7 2.2 collective-permute-start.23
  826.9 2.0 collective-permute-start.22
  828.9 2.1 collective-permute-start.21
  833.0 1.9 collective-permute-start.19
  834.9 4.7 collective-permute-start.18
  843.5 1.9 collective-permute-start.15
  845.4 2.5 collective-permute-start.14
  847.9 2.5 collective-permute-start.13
  850.4 2.0 collective-permute-start.12
  852.5 1.9 collective-permute-start.11
  854.4 4.0 collective-permute-start.10
  858.5 3.1 collective-permute-start.9
  861.6 17.3 %collective-permute-start.8 = (f32[24,512]{1,0:T(8,128)S(1)}, f32[24,512]{1,0:T(8,128)S(1)}, u32[]{:S(2)}, u32[]{:S(2)}) collective-permute-start(f32[24,512]{1,0:T(8,128)S(1)} %fusion), channel_id=1, source_target_pairs={{0,9},{1,10},{2,11},{3,12},{4,13},{5,14},{6,15},{7,16},{8,17},{9,1... | collective-permute-start | bytes 147464
  878.9 13.1 %collective-permute-start.7 = (f32[24,512]{1,0:T(8,128)S(1)}, f32[24,512]{1,0:T(8,128)S(1)}, u32[]{:S(2)}, u32[]{:S(2)}) collective-permute-start(f32[24,512]{1,0:T(8,128)S(1)} %fusion), channel_id=1, source_target_pairs={{0,8},{1,9},{2,10},{3,11},{4,12},{5,13},{6,14},{7,15},{8,16},{9,17... | collective-permute-start | bytes 147464
  892.1 13.1 %collective-permute-start.6 = (f32[24,512]{1,0:T(8,128)S(1)}, f32[24,512]{1,0:T(8,128)S(1)}, u32[]{:S(2)}, u32[]{:S(2)}) collective-permute-start(f32[24,512]{1,0:T(8,128)S(1)} %fusion), channel_id=1, source_target_pairs={{0,7},{1,8},{2,9},{3,10},{4,11},{5,12},{6,13},{7,14},{8,15},{9,16}... | collective-permute-start | bytes 147464
  905.2 13.1 %collective-permute-start.5 = (f32[24,512]{1,0:T(8,128)S(1)}, f32[24,512]{1,0:T(8,128)S(1)}, u32[]{:S(2)}, u32[]{:S(2)}) collective-permute-start(f32[24,512]{1,0:T(8,128)S(1)} %fusion), channel_id=1, source_target_pairs={{0,6},{1,7},{2,8},{3,9},{4,10},{5,11},{6,12},{7,13},{8,14},{9,15},... | collective-permute-start | bytes 147464
  918.4 13.1 %collective-permute-start.4 = (f32[24,512]{1,0:T(8,128)S(1)}, f32[24,512]{1,0:T(8,128)S(1)}, u32[]{:S(2)}, u32[]{:S(2)}) collective-permute-start(f32[24,512]{1,0:T(8,128)S(1)} %fusion), channel_id=1, source_target_pairs={{0,5},{1,6},{2,7},{3,8},{4,9},{5,10},{6,11},{7,12},{8,13},{9,14},{... | collective-permute-start | bytes 147464
  931.5 13.1 %collective-permute-start.3 = (f32[24,512]{1,0:T(8,128)S(1)}, f32[24,512]{1,0:T(8,128)S(1)}, u32[]{:S(2)}, u32[]{:S(2)}) collective-permute-start(f32[24,512]{1,0:T(8,128)S(1)} %fusion), channel_id=1, source_target_pairs={{0,4},{1,5},{2,6},{3,7},{4,8},{5,9},{6,10},{7,11},{8,12},{9,13},{1... | collective-permute-start | bytes 147464
  944.7 13.1 %collective-permute-start.2 = (f32[24,512]{1,0:T(8,128)S(1)}, f32[24,512]{1,0:T(8,128)S(1)}, u32[]{:S(2)}, u32[]{:S(2)}) collective-permute-start(f32[24,512]{1,0:T(8,128)S(1)} %fusion), channel_id=1, source_target_pairs={{0,3},{1,4},{2,5},{3,6},{4,7},{5,8},{6,9},{7,10},{8,11},{9,12},{10... | collective-permute-start | bytes 147464
  957.8 13.1 %collective-permute-start.1 = (f32[24,512]{1,0:T(8,128)S(1)}, f32[24,512]{1,0:T(8,128)S(1)}, u32[]{:S(2)}, u32[]{:S(2)}) collective-permute-start(f32[24,512]{1,0:T(8,128)S(1)} %fusion), channel_id=1, source_target_pairs={{0,2},{1,3},{2,4},{3,5},{4,6},{5,7},{6,8},{7,9},{8,10},{9,11},{10,... | collective-permute-start | bytes 147464
  971.0 13.1 %collective-permute-start = (f32[24,512]{1,0:T(8,128)S(1)}, f32[24,512]{1,0:T(8,128)}, u32[]{:S(2)}, u32[]{:S(2)}) collective-permute-start(f32[24,512]{1,0:T(8,128)S(1)} %fusion), channel_id=1, source_target_pairs={{0,1},{1,2},{2,3},{3,4},{4,5},{5,6},{6,7},{7,8},{8,9},{9,10},{10,1... | collective-permute-start | bytes 147464
  985.5 5.5 collective-permute-done
  991.0 17.0 %concatenate = f32[1044,512]{1,0:T(8,128)S(1)} concatenate(f32[12,512]{1,0:T(8,128)S(1)} %collective-permute-done.42, f32[24,512]{1,0:T(8,128)S(1)} %collective-permute-done.41, f32[24,512]{1,0:T(8,128)S(1)} %collective-permute-done.40, f32[24,512]{1,0:T(8,128)S(1)} %collective-permute-done.39, f32[24,512]{1,0:T(8,128)S(1)} %collective-permute-done.38, ...), dimensions={0} | concatenate | bytes 4276224
  1008.7 9.1 reshape.68
  1017.8 4.5 fusion.8
  1023.9 74.4 %all-reduce.1 = f32[5120]{0:T(1024)S(1)} all-reduce(f32[5120]{0:T(1024)S(1)} %fusion.8), channel_id=3, replica_groups=mesh['dp'=16,'group'=16] {'dp','group'}, use_global_device_ids=true, to_apply=%region_5.6.clone | all-reduce | flops 5120 | bytes 40960
  (98 shorter events, 13.0 us)
Async XLA Ops:
  7.2 1001.5 %all-gather.3.cloned.1.call-start = ((), (), s32[]{:S(2)}) async-start(), calls=%async_computation | async-start | bytes 6316032 | tf_op jit(solution)/shard_map/all_gather | solution.py:32
  731.4 20.5 %collective-permute-start.41 = (f32[24,512]{1,0:T(8,128)S(1)}, f32[24,512]{1,0:T(8,128)S(1)}, u32[]{:S(2)}, u32[]{:S(2)}) collective-permute-start(f32[24,512]{1,0:T(8,128)S(1)} %fusion), channel_id=1, source_target_pairs={{0,42},{1,43},{2,44},{3,45},{4,46},{5,47},{6,48},{7,49},{8,50},{9,... | collective-permute-start | bytes 147464
  733.3 29.4 %collective-permute-start.40 = (f32[24,512]{1,0:T(8,128)S(1)}, f32[24,512]{1,0:T(8,128)S(1)}, u32[]{:S(2)}, u32[]{:S(2)}) collective-permute-start(f32[24,512]{1,0:T(8,128)S(1)} %fusion), channel_id=1, source_target_pairs={{0,41},{1,42},{2,43},{3,44},{4,45},{5,46},{6,47},{7,48},{8,49},{9,... | collective-permute-start | bytes 147464
  735.3 12.5 %collective-permute-start.42 = (f32[12,512]{1,0:T(8,128)S(1)}, f32[12,512]{1,0:T(8,128)S(1)}, u32[]{:S(2)}, u32[]{:S(2)}) collective-permute-start(f32[12,512]{1,0:T(8,128)S(1)} %slice), channel_id=1, source_target_pairs={{0,43},{1,44},{2,45},{3,46},{4,47},{5,48},{6,49},{7,50},{8,51},{9,... | collective-permute-start | bytes 73736
  743.9 23.4 %collective-permute-start.39 = (f32[24,512]{1,0:T(8,128)S(1)}, f32[24,512]{1,0:T(8,128)S(1)}, u32[]{:S(2)}, u32[]{:S(2)}) collective-permute-start(f32[24,512]{1,0:T(8,128)S(1)} %fusion), channel_id=1, source_target_pairs={{0,40},{1,41},{2,42},{3,43},{4,44},{5,45},{6,46},{7,47},{8,48},{9,... | collective-permute-start | bytes 147464
  745.9 29.5 %collective-permute-start.38 = (f32[24,512]{1,0:T(8,128)S(1)}, f32[24,512]{1,0:T(8,128)S(1)}, u32[]{:S(2)}, u32[]{:S(2)}) collective-permute-start(f32[24,512]{1,0:T(8,128)S(1)} %fusion), channel_id=1, source_target_pairs={{0,39},{1,40},{2,41},{3,42},{4,43},{5,44},{6,45},{7,46},{8,47},{9,... | collective-permute-start | bytes 147464
  747.8 53.8 %collective-permute-start.37 = (f32[24,512]{1,0:T(8,128)S(1)}, f32[24,512]{1,0:T(8,128)S(1)}, u32[]{:S(2)}, u32[]{:S(2)}) collective-permute-start(f32[24,512]{1,0:T(8,128)S(1)} %fusion), channel_id=1, source_target_pairs={{0,38},{1,39},{2,40},{3,41},{4,42},{5,43},{6,44},{7,45},{8,46},{9,... | collective-permute-start | bytes 147464
  751.9 51.6 %collective-permute-start.36 = (f32[24,512]{1,0:T(8,128)S(1)}, f32[24,512]{1,0:T(8,128)S(1)}, u32[]{:S(2)}, u32[]{:S(2)}) collective-permute-start(f32[24,512]{1,0:T(8,128)S(1)} %fusion), channel_id=1, source_target_pairs={{0,37},{1,38},{2,39},{3,40},{4,41},{5,42},{6,43},{7,44},{8,45},{9,... | collective-permute-start | bytes 147464
  762.7 43.4 %collective-permute-start.35 = (f32[24,512]{1,0:T(8,128)S(1)}, f32[24,512]{1,0:T(8,128)S(1)}, u32[]{:S(2)}, u32[]{:S(2)}) collective-permute-start(f32[24,512]{1,0:T(8,128)S(1)} %fusion), channel_id=1, source_target_pairs={{0,36},{1,37},{2,38},{3,39},{4,40},{5,41},{6,42},{7,43},{8,44},{9,... | collective-permute-start | bytes 147464
  767.3 44.6 %collective-permute-start.34 = (f32[24,512]{1,0:T(8,128)S(1)}, f32[24,512]{1,0:T(8,128)S(1)}, u32[]{:S(2)}, u32[]{:S(2)}) collective-permute-start(f32[24,512]{1,0:T(8,128)S(1)} %fusion), channel_id=1, source_target_pairs={{0,35},{1,36},{2,37},{3,38},{4,39},{5,40},{6,41},{7,42},{8,43},{9,... | collective-permute-start | bytes 147464
  775.4 38.5 %collective-permute-start.33 = (f32[24,512]{1,0:T(8,128)S(1)}, f32[24,512]{1,0:T(8,128)S(1)}, u32[]{:S(2)}, u32[]{:S(2)}) collective-permute-start(f32[24,512]{1,0:T(8,128)S(1)} %fusion), channel_id=1, source_target_pairs={{0,34},{1,35},{2,36},{3,37},{4,38},{5,39},{6,40},{7,41},{8,42},{9,... | collective-permute-start | bytes 147464
  801.6 14.3 %collective-permute-start.32 = (f32[24,512]{1,0:T(8,128)S(1)}, f32[24,512]{1,0:T(8,128)S(1)}, u32[]{:S(2)}, u32[]{:S(2)}) collective-permute-start(f32[24,512]{1,0:T(8,128)S(1)} %fusion), channel_id=1, source_target_pairs={{0,33},{1,34},{2,35},{3,36},{4,37},{5,38},{6,39},{7,40},{8,41},{9,... | collective-permute-start | bytes 147464
  803.6 14.2 %collective-permute-start.31 = (f32[24,512]{1,0:T(8,128)S(1)}, f32[24,512]{1,0:T(8,128)S(1)}, u32[]{:S(2)}, u32[]{:S(2)}) collective-permute-start(f32[24,512]{1,0:T(8,128)S(1)} %fusion), channel_id=1, source_target_pairs={{0,32},{1,33},{2,34},{3,35},{4,36},{5,37},{6,38},{7,39},{8,40},{9,... | collective-permute-start | bytes 147464
  806.1 14.5 %collective-permute-start.30 = (f32[24,512]{1,0:T(8,128)S(1)}, f32[24,512]{1,0:T(8,128)S(1)}, u32[]{:S(2)}, u32[]{:S(2)}) collective-permute-start(f32[24,512]{1,0:T(8,128)S(1)} %fusion), channel_id=1, source_target_pairs={{0,31},{1,32},{2,33},{3,34},{4,35},{5,36},{6,37},{7,38},{8,39},{9,... | collective-permute-start | bytes 147464
  812.0 10.6 collective-permute-start.29
  813.9 10.8 collective-permute-start.28
  815.8 11.0 collective-permute-start.27
  817.8 11.1 %collective-permute-start.26 = (f32[24,512]{1,0:T(8,128)S(1)}, f32[24,512]{1,0:T(8,128)S(1)}, u32[]{:S(2)}, u32[]{:S(2)}) collective-permute-start(f32[24,512]{1,0:T(8,128)S(1)} %fusion), channel_id=1, source_target_pairs={{0,27},{1,28},{2,29},{3,30},{4,31},{5,32},{6,33},{7,34},{8,35},{9,... | collective-permute-start | bytes 147464
  820.6 10.4 collective-permute-start.25
  822.5 10.4 collective-permute-start.24
  824.7 10.3 collective-permute-start.23
  826.9 12.7 %collective-permute-start.22 = (f32[24,512]{1,0:T(8,128)S(1)}, f32[24,512]{1,0:T(8,128)S(1)}, u32[]{:S(2)}, u32[]{:S(2)}) collective-permute-start(f32[24,512]{1,0:T(8,128)S(1)} %fusion), channel_id=1, source_target_pairs={{0,23},{1,24},{2,25},{3,26},{4,27},{5,28},{6,29},{7,30},{8,31},{9,... | collective-permute-start | bytes 147464
  828.9 12.6 %collective-permute-start.21 = (f32[24,512]{1,0:T(8,128)S(1)}, f32[24,512]{1,0:T(8,128)S(1)}, u32[]{:S(2)}, u32[]{:S(2)}) collective-permute-start(f32[24,512]{1,0:T(8,128)S(1)} %fusion), channel_id=1, source_target_pairs={{0,22},{1,23},{2,24},{3,25},{4,26},{5,27},{6,28},{7,29},{8,30},{9,... | collective-permute-start | bytes 147464
  831.1 12.4 %collective-permute-start.20 = (f32[24,512]{1,0:T(8,128)S(1)}, f32[24,512]{1,0:T(8,128)S(1)}, u32[]{:S(2)}, u32[]{:S(2)}) collective-permute-start(f32[24,512]{1,0:T(8,128)S(1)} %fusion), channel_id=1, source_target_pairs={{0,21},{1,22},{2,23},{3,24},{4,25},{5,26},{6,27},{7,28},{8,29},{9,... | collective-permute-start | bytes 147464
  833.0 12.4 %collective-permute-start.19 = (f32[24,512]{1,0:T(8,128)S(1)}, f32[24,512]{1,0:T(8,128)S(1)}, u32[]{:S(2)}, u32[]{:S(2)}) collective-permute-start(f32[24,512]{1,0:T(8,128)S(1)} %fusion), channel_id=1, source_target_pairs={{0,20},{1,21},{2,22},{3,23},{4,24},{5,25},{6,26},{7,27},{8,28},{9,... | collective-permute-start | bytes 147464
  834.9 13.0 %collective-permute-start.18 = (f32[24,512]{1,0:T(8,128)S(1)}, f32[24,512]{1,0:T(8,128)S(1)}, u32[]{:S(2)}, u32[]{:S(2)}) collective-permute-start(f32[24,512]{1,0:T(8,128)S(1)} %fusion), channel_id=1, source_target_pairs={{0,19},{1,20},{2,21},{3,22},{4,23},{5,24},{6,25},{7,26},{8,27},{9,... | collective-permute-start | bytes 147464
  839.6 10.8 collective-permute-start.17
  841.5 10.9 collective-permute-start.16
  843.5 10.9 collective-permute-start.15
  845.4 13.0 %collective-permute-start.14 = (f32[24,512]{1,0:T(8,128)S(1)}, f32[24,512]{1,0:T(8,128)S(1)}, u32[]{:S(2)}, u32[]{:S(2)}) collective-permute-start(f32[24,512]{1,0:T(8,128)S(1)} %fusion), channel_id=1, source_target_pairs={{0,15},{1,16},{2,17},{3,18},{4,19},{5,20},{6,21},{7,22},{8,23},{9,... | collective-permute-start | bytes 147464
  847.9 13.6 %collective-permute-start.13 = (f32[24,512]{1,0:T(8,128)S(1)}, f32[24,512]{1,0:T(8,128)S(1)}, u32[]{:S(2)}, u32[]{:S(2)}) collective-permute-start(f32[24,512]{1,0:T(8,128)S(1)} %fusion), channel_id=1, source_target_pairs={{0,14},{1,15},{2,16},{3,17},{4,18},{5,19},{6,20},{7,21},{8,22},{9,... | collective-permute-start | bytes 147464
  850.4 28.5 %collective-permute-start.12 = (f32[24,512]{1,0:T(8,128)S(1)}, f32[24,512]{1,0:T(8,128)S(1)}, u32[]{:S(2)}, u32[]{:S(2)}) collective-permute-start(f32[24,512]{1,0:T(8,128)S(1)} %fusion), channel_id=1, source_target_pairs={{0,13},{1,14},{2,15},{3,16},{4,17},{5,18},{6,19},{7,20},{8,21},{9,... | collective-permute-start | bytes 147464
  852.5 39.6 %collective-permute-start.11 = (f32[24,512]{1,0:T(8,128)S(1)}, f32[24,512]{1,0:T(8,128)S(1)}, u32[]{:S(2)}, u32[]{:S(2)}) collective-permute-start(f32[24,512]{1,0:T(8,128)S(1)} %fusion), channel_id=1, source_target_pairs={{0,12},{1,13},{2,14},{3,15},{4,16},{5,17},{6,18},{7,19},{8,20},{9,... | collective-permute-start | bytes 147464
  854.4 50.8 %collective-permute-start.10 = (f32[24,512]{1,0:T(8,128)S(1)}, f32[24,512]{1,0:T(8,128)S(1)}, u32[]{:S(2)}, u32[]{:S(2)}) collective-permute-start(f32[24,512]{1,0:T(8,128)S(1)} %fusion), channel_id=1, source_target_pairs={{0,11},{1,12},{2,13},{3,14},{4,15},{5,16},{6,17},{7,18},{8,19},{9,... | collective-permute-start | bytes 147464
  858.5 112.5 %copy-start.4 = (f32[24,512]{1,0:T(8,128)}, f32[24,512]{1,0:T(8,128)S(1)}, u32[]{:S(2)}) copy-start(f32[24,512]{1,0:T(8,128)S(1)} %collective-permute-done.14) | copy-start | bytes 147460
  858.5 59.9 %collective-permute-start.9 = (f32[24,512]{1,0:T(8,128)S(1)}, f32[24,512]{1,0:T(8,128)S(1)}, u32[]{:S(2)}, u32[]{:S(2)}) collective-permute-start(f32[24,512]{1,0:T(8,128)S(1)} %fusion), channel_id=1, source_target_pairs={{0,10},{1,11},{2,12},{3,13},{4,14},{5,15},{6,16},{7,17},{8,18},{9,... | collective-permute-start | bytes 147464
  861.6 122.5 %copy-start.5 = (f32[24,512]{1,0:T(8,128)}, f32[24,512]{1,0:T(8,128)S(1)}, u32[]{:S(2)}) copy-start(f32[24,512]{1,0:T(8,128)S(1)} %collective-permute-done.13) | copy-start | bytes 147460
  861.6 69.9 %collective-permute-start.8 = (f32[24,512]{1,0:T(8,128)S(1)}, f32[24,512]{1,0:T(8,128)S(1)}, u32[]{:S(2)}, u32[]{:S(2)}) collective-permute-start(f32[24,512]{1,0:T(8,128)S(1)} %fusion), channel_id=1, source_target_pairs={{0,9},{1,10},{2,11},{3,12},{4,13},{5,14},{6,15},{7,16},{8,17},{9,1... | collective-permute-start | bytes 147464
  878.9 105.2 %copy-start.6 = (f32[24,512]{1,0:T(8,128)}, f32[24,512]{1,0:T(8,128)S(1)}, u32[]{:S(2)}) copy-start(f32[24,512]{1,0:T(8,128)S(1)} %collective-permute-done.12) | copy-start | bytes 147460
  878.9 65.7 %collective-permute-start.7 = (f32[24,512]{1,0:T(8,128)S(1)}, f32[24,512]{1,0:T(8,128)S(1)}, u32[]{:S(2)}, u32[]{:S(2)}) collective-permute-start(f32[24,512]{1,0:T(8,128)S(1)} %fusion), channel_id=1, source_target_pairs={{0,8},{1,9},{2,10},{3,11},{4,12},{5,13},{6,14},{7,15},{8,16},{9,17... | collective-permute-start | bytes 147464
  892.0 92.1 %copy-start.7 = (f32[24,512]{1,0:T(8,128)}, f32[24,512]{1,0:T(8,128)S(1)}, u32[]{:S(2)}) copy-start(f32[24,512]{1,0:T(8,128)S(1)} %collective-permute-done.11) | copy-start | bytes 147460
  892.1 65.7 %collective-permute-start.6 = (f32[24,512]{1,0:T(8,128)S(1)}, f32[24,512]{1,0:T(8,128)S(1)}, u32[]{:S(2)}, u32[]{:S(2)}) collective-permute-start(f32[24,512]{1,0:T(8,128)S(1)} %fusion), channel_id=1, source_target_pairs={{0,7},{1,8},{2,9},{3,10},{4,11},{5,12},{6,13},{7,14},{8,15},{9,16}... | collective-permute-start | bytes 147464
  905.2 65.7 %collective-permute-start.5 = (f32[24,512]{1,0:T(8,128)S(1)}, f32[24,512]{1,0:T(8,128)S(1)}, u32[]{:S(2)}, u32[]{:S(2)}) collective-permute-start(f32[24,512]{1,0:T(8,128)S(1)} %fusion), channel_id=1, source_target_pairs={{0,6},{1,7},{2,8},{3,9},{4,10},{5,11},{6,12},{7,13},{8,14},{9,15},... | collective-permute-start | bytes 147464
  918.4 65.8 %collective-permute-start.4 = (f32[24,512]{1,0:T(8,128)S(1)}, f32[24,512]{1,0:T(8,128)S(1)}, u32[]{:S(2)}, u32[]{:S(2)}) collective-permute-start(f32[24,512]{1,0:T(8,128)S(1)} %fusion), channel_id=1, source_target_pairs={{0,5},{1,6},{2,7},{3,8},{4,9},{5,10},{6,11},{7,12},{8,13},{9,14},{... | collective-permute-start | bytes 147464
  931.5 52.7 %collective-permute-start.3 = (f32[24,512]{1,0:T(8,128)S(1)}, f32[24,512]{1,0:T(8,128)S(1)}, u32[]{:S(2)}, u32[]{:S(2)}) collective-permute-start(f32[24,512]{1,0:T(8,128)S(1)} %fusion), channel_id=1, source_target_pairs={{0,4},{1,5},{2,6},{3,7},{4,8},{5,9},{6,10},{7,11},{8,12},{9,13},{1... | collective-permute-start | bytes 147464
  944.7 39.6 %collective-permute-start.2 = (f32[24,512]{1,0:T(8,128)S(1)}, f32[24,512]{1,0:T(8,128)S(1)}, u32[]{:S(2)}, u32[]{:S(2)}) collective-permute-start(f32[24,512]{1,0:T(8,128)S(1)} %fusion), channel_id=1, source_target_pairs={{0,3},{1,4},{2,5},{3,6},{4,7},{5,8},{6,9},{7,10},{8,11},{9,12},{10... | collective-permute-start | bytes 147464
  957.8 26.5 %collective-permute-start.1 = (f32[24,512]{1,0:T(8,128)S(1)}, f32[24,512]{1,0:T(8,128)S(1)}, u32[]{:S(2)}, u32[]{:S(2)}) collective-permute-start(f32[24,512]{1,0:T(8,128)S(1)} %fusion), channel_id=1, source_target_pairs={{0,2},{1,3},{2,4},{3,5},{4,6},{5,7},{6,8},{7,9},{8,10},{9,11},{10,... | collective-permute-start | bytes 147464
  971.0 20.0 %collective-permute-start = (f32[24,512]{1,0:T(8,128)S(1)}, f32[24,512]{1,0:T(8,128)}, u32[]{:S(2)}, u32[]{:S(2)}) collective-permute-start(f32[24,512]{1,0:T(8,128)S(1)} %fusion), channel_id=1, source_target_pairs={{0,1},{1,2},{2,3},{3,4},{4,5},{5,6},{6,7},{7,8},{8,9},{9,10},{10,1... | collective-permute-start | bytes 147464
  (18 other events, 325.6 us)
Sparse Core Ops, SparseCore 0:
  11.8 117.4 all-gather.2
where the time goes:
time: 1110 us
  blocking collectives  785 us (71%)
  starting transfers between devices  252 us (23%)
  local copies, waits for them, and re-layouts  29.2 us (3%)
  between operations  19 us (2%)
  matrix products  13.1 us (1%)
    unnamed x2, blocking collectives  751 us
    unnamed x43, starting transfers between devices  252 us
    psum x1, blocking collectives, body(): lax.psum((jnp.sum(scores, axis=1, keepdims=True), jnp.sum(scores * scores...  33.9 us
    unnamed x49, local copies, waits for them, and re-layouts  29.2 us
  transfers between devices with their start and end apart: 44, of which 1 were waited for; matrix products, arithmetic and copies ran while one was open for 64% of the time, Pallas kernels for 0%

commit v1 on v0

--- a/solution.py
+++ b/solution.py
@@ -8,7 +8,10 @@
     prompts, answers, length, features = hidden_in.shape
     kv_width = value_weight.shape[1]
     row_count = prompts * answers * length
-    group_count = answers * lax.axis_size("group")
+    n_dp = lax.axis_size("dp")
+    n_group = lax.axis_size("group")
+    group_count = answers * n_group
+    shard_rows = value_weight.shape[0]
     scores = rewards.astype(jnp.float32)
     reward_sum, square_sum = lax.psum(
         (jnp.sum(scores, axis=1, keepdims=True), jnp.sum(scores * scores, axis=1, keepdims=True)),
@@ -29,22 +32,30 @@
         token_weight.reshape(row_count, 1)
         * value_cot.reshape(row_count, kv_width).astype(jnp.float32)
     ).astype(jnp.bfloat16)
-    full_weight = lax.all_gather(value_weight, ("dp", "group"), axis=0, tiled=True)
+    part = lax.all_gather(value_weight[None], "group", axis=0, tiled=True)
+    full_weight = lax.all_gather(part[None], "dp", axis=0, tiled=True).reshape(features, kv_width)
     projected = jnp.dot(normed, full_weight, preferred_element_type=jnp.float32)
     back = lax.dot_general(
         scaled_cot, full_weight, (((1,), (1,)), ((), ())), preferred_element_type=jnp.float32
     )
     gain_term = jnp.sum(back * (flat_in.astype(jnp.float32) * inverse), axis=0)
     values = projected.astype(jnp.bfloat16).reshape(prompts, answers, length, kv_width)
-    gain_grad = lax.psum_scatter(gain_term, ("dp", "group"), scatter_dimension=0, tiled=True)
-    weight_grad = lax.psum_scatter(
-        lax.dot_general(
-            normed, scaled_cot, (((0,), (0,)), ((), ())), preferred_element_type=jnp.float32
-        ),
-        ("dp", "group"),
-        scatter_dimension=0,
-        tiled=True,
+    grad_part = lax.dot_general(
+        normed, scaled_cot, (((0,), (0,)), ((), ())), preferred_element_type=jnp.float32
     )
+    block = shard_rows * kv_width
+    pad = (-shard_rows) % 128
+    payload = jnp.concatenate(
+        [
+            grad_part.reshape(n_dp, n_group, block),
+            jnp.pad(gain_term.reshape(n_dp, n_group, shard_rows), ((0, 0), (0, 0), (0, pad))),
+        ],
+        axis=2,
+    )
+    payload = lax.psum_scatter(payload, "dp", scatter_dimension=0, tiled=True)
+    payload = lax.psum_scatter(payload.reshape(n_group, -1), "group", scatter_dimension=0, tiled=True)
+    weight_grad = payload[0, :block].reshape(shard_rows, kv_width)
+    gain_grad = payload[0, block:block + shard_rows]
     return (values, weight_grad, gain_grad)
 
 

time: 1110 us -> 308 us (0.28)
  blocking collectives: 785 us -> 50.5 us
  starting transfers between devices: 252 us -> 0.12 us
  waiting for transfers between devices: 6.3 us -> 177 us
    unnamed x2 -> x0, blocking collectives: 751 us -> none
    unnamed x43 -> x1, starting transfers between devices: 252 us -> 0.04 us
    unnamed x44 -> x4, waiting for transfers between devices: 6.28 us -> 92.6 us
    reduce_scatter x0 -> x1, waiting for transfers between devices: none -> 83.9 us  [body(): payload = lax.psum_scatter(payload, 'dp', scatter_dimension=0, tiled=True)]
    unnamed x49 -> x9, local copies, waits for them, and re-layouts: 29.2 us -> 0.67 us
    reshape x0 -> x3, local copies, waits for them, and re-layouts: none -> 21.6 us  [the longest x1 12.5 us: body(): grad_part.reshape(n_dp, n_group, block)]
    all_gather x0 -> x1, blocking collectives: none -> 19.2 us  [body(): part = lax.all_gather(value_weight[None], 'group', axis=0, tiled=True)]
  transfers between devices with their start and end apart: 44 -> 3, of which waited for: 1 -> 2; matrix products, arithmetic and copies ran while one was open for 64% -> 8% of each run, Pallas kernels for 0% -> 0%
where the time goes in v1:
time: 308 us; the launch traced here: 305 us
  waiting for transfers between devices  177 us (57%)
  blocking collectives  50.5 us (16%)
  local copies, waits for them, and re-layouts  35.6 us (12%)
  between operations  17.8 us (6%)
  matrix products  14 us (5%)
  other arithmetic  10.5 us (3%)
    unnamed x4, waiting for transfers between devices  92.6 us
    reduce_scatter x1, waiting for transfers between devices, body(): payload = lax.psum_scatter(payload, 'dp', scatter_dimension=0, tiled=True)  83.9 us
    psum x1, blocking collectives, body(): lax.psum((jnp.sum(scores, axis=1, keepdims=True), jnp.sum(scores * scores...  31.4 us
    all_gather x1, blocking collectives, body(): part = lax.all_gather(value_weight[None], 'group', axis=0, tiled=True)  19.2 us
    reshape x1, local copies, waits for them, and re-layouts, body(): grad_part.reshape(n_dp, n_group, block)  12.5 us
    reshape x1, local copies, waits for them, and re-layouts, body(): lax.all_gather(part[None], 'dp', axis=0, tiled=True)  8.97 us
    concatenate x1, other arithmetic, body(): jnp.concatenate([grad_part.reshape(n_dp, n_group, block), jnp.pad(gain_te...  8.76 us
    all_gather x1, local copies, waits for them, and re-layouts, body(): lax.all_gather(part[None], 'dp', axis=0, tiled=True)  8.16 us
  transfers between devices with their start and end apart: 3, of which 2 were waited for; matrix products, arithmetic and copies ran while one was open for 8% of the time, Pallas kernels for 0%

profile of v1, /device:TPU:97, one launch (start us, length us, event | category | flops | bytes accessed | tf_op | source)
XLA Modules:
  0.0 305.1 jit_solution(9213399940424357688)
XLA Ops:
  7.2 0.0 copy-start
  7.2 0.0 copy-start.2
  7.2 0.0 copy-start.1
  7.2 0.0 all-gather.5.cloned.1.call-start
  7.2 19.2 %all-gather.2 = bf16[16,20,512]{2,1,0:T(8,128)(2,1)S(1)} all-gather(bf16[1,20,512]{2,1,0:T(8,128)(2,1)} %bitcast.33), channel_id=2, replica_groups=mesh['dp'=16,'group'=16] {'group'}, dimensions={0}, use_global_device_ids=true | all-gather | bytes 348160 | tf_op jit(solution)/shard_map/all_gather | solution.py:35
  26.4 0.8 copy.9
  27.2 0.0 all-gather.5.cloned.1.call-update
  27.2 0.0 reduce-scatter.2.cloned.1.call-start
  27.9 31.4 %all-reduce.2 = (f32[1,1]{1,0:T(1,128)}, f32[1,1]{1,0:T(1,128)}) all-reduce(f32[1,1]{1,0:T(1,128)S(6)} %convert_element_type.48, f32[1,1]{1,0:T(1,128)S(6)} %mul.53), channel_id=1, replica_groups=mesh['dp'=16,'group'=16] {'group'}, use_global_device_ids=true, to_apply=%region_1.0 | all-reduce | flops 2 | bytes 16 | tf_op jit(solution)/shard_map/psum | solution.py:16
  62.7 1.7 fusion.2
  64.4 0.0 copy-done
  64.4 0.0 copy-done.2
  64.4 0.0 copy-done.1
  64.4 5.6 %fusion.8 = f32[5120,512]{1,0:T(8,128)} fusion(bf16[1,1,128,5120]{3,2,1,0:T(8,128)(2,1)S(1)} %copy-done, f32[5120]{0:T(1024)S(1)} %copy-done.2, f32[128]{0:T(128)S(1)} %get-tuple-element.6, bf16[1,1,128,512]{3,2,1,0:T(8,128)(2,1)S(1)} %copy-done.1, f32[128]{0:T(128)S(1)} %get-tuple-element.5), kind=kOutput, calls=%fused_computation.14 | convolution fusion | flops 673906688 | bytes 11949056 | tf_op jit(solution)/shard_map/dot_general | solution.py:43
  70.0 12.5 %reshape.98 = f32[16,16,10240]{2,1,0:T(8,128)} reshape(f32[5120,512]{1,0:T(8,128)} %fusion.8) | data formatting | bytes 20971520 | tf_op jit(solution)/shard_map/reshape | solution.py:50
  82.5 0.0 all-gather.5.cloned.1.call-done
  82.5 8.2 %copy.10 = bf16[256,20,512]{2,1,0:T(8,128)(2,1)} copy(bf16[256,20,512]{2,0,1:T(8,128)(2,1)} %all-gather.5.cloned.1.call-done) | data formatting | bytes 10485760 | tf_op jit(solution)/shard_map/all_gather | solution.py:36
  90.7 9.0 %reshape.96 = bf16[5120,512]{1,0:T(8,128)(2,1)} reshape(bf16[256,20,512]{2,1,0:T(8,128)(2,1)} %copy.10) | data formatting | bytes 10485760 | tf_op jit(solution)/shard_map/reshape | solution.py:36
  99.7 4.3 %fusion.5 = f32[5120]{0:T(1024)S(1)} fusion(bf16[1,1,128,5120]{3,2,1,0:T(8,128)(2,1)S(1)} %copy-done, bf16[5120,512]{1,0:T(8,128)(2,1)} %reshape.96, f32[128]{0:T(128)S(1)} %get-tuple-element.6, bf16[1,1,128,512]{3,2,1,0:T(8,128)(2,1)S(1)} %copy-done.1, f32[128]{0:T(128)S(1)} %get-tuple-element.5), kind=kOutput, calls=%fused_computation.10 | convolution fusion | flops 673901568 | bytes 6706176 | tf_op jit(solution)/shard_map/dot_general | solution.py:38
  104.0 0.1 reshape.99
  104.1 8.8 %select_maximum_fusion = f32[16,16,10368]{2,1,0:T(8,128)} fusion(f32[16,16,20]{2,1,0:T(8,128)S(1)} %reshape.99, f32[16,16,10240]{2,1,0:T(8,128)} %reshape.98), kind=kLoop, calls=%fused_computation | loop fusion | flops 7962624 | bytes 21123072 | tf_op jit(solution)/shard_map/concatenate | solution.py:48
  112.9 0.0 copy-start.3
  112.9 0.0 reduce-scatter.2.cloned.1.call-update
  112.9 0.0 all-reduce.5.cloned.1.call-start
  113.0 83.9 %reduce-scatter.2.cloned.1.call-done = f32[1,16,10368]{2,1,0:T(8,128)} async-done(((f32[16,16,10368]{2,1,0:T(8,128)}), f32[1,16,10368]{2,1,0:T(8,128)}) %reduce-scatter.2.cloned.1.call-update) | async-done | bytes 663568 | tf_op jit(solution)/shard_map/reduce_scatter | solution.py:55
  196.9 0.0 all-reduce.5.cloned.1.call-update
  196.9 0.0 copy-done.3
  196.9 0.7 dynamic-slice
  197.6 4.0 %fusion.7 = bf16[1,1,128,512]{3,2,1,0:T(8,128)(2,1)} fusion(bf16[5120,512]{1,0:T(8,128)(2,1)} %reshape.96, bf16[1,1,128,5120]{3,2,1,0:T(8,128)(2,1)S(1)} %copy-done, f32[5120]{0:T(1024)S(1)} %copy-done.2, f32[128]{0:T(128)S(1)} %get-tuple-element.6), kind=kOutput, calls=%fused_computation.13 | convolution fusion | flops 673775616 | bytes 6705664 | tf_op jit(solution)/shard_map/dot_general | solution.py:37
  201.6 92.6 %all-reduce.5.cloned.1.call-done = f32[16,10368]{1,0:T(8,128)} async-done(((f32[16,10368]{1,0:T(8,128)}), f32[16,10368]{1,0:T(8,128)}) %all-reduce.5.cloned.1.call-update) | async-done | bytes 663568
  294.2 1.8 dynamic-slice_reduce_fusion
  296.0 0.6 reshape_squeeze.3
  296.6 1.9 dynamic-slice_bitcast_fusion
  (1 shorter events, 0.0 us)
Async XLA Ops:
  7.2 57.2 %copy-start = (bf16[1,1,128,5120]{3,2,1,0:T(8,128)(2,1)S(1)}, bf16[1,1,128,5120]{3,2,1,0:T(8,128)(2,1)}, u32[]{:S(2)}) copy-start(bf16[1,1,128,5120]{3,2,1,0:T(8,128)(2,1)} %param.6) | copy-start | bytes 3932164
  7.2 57.2 %copy-start.2 = (f32[5120]{0:T(1024)S(1)}, f32[5120]{0:T(1024)}, u32[]{:S(2)}) copy-start(f32[5120]{0:T(1024)} %param.7) | copy-start | bytes 61444
  7.2 57.2 %copy-start.1 = (bf16[1,1,128,512]{3,2,1,0:T(8,128)(2,1)S(1)}, bf16[1,1,128,512]{3,2,1,0:T(8,128)(2,1)}, u32[]{:S(2)}) copy-start(bf16[1,1,128,512]{3,2,1,0:T(8,128)(2,1)} %param.9) | copy-start | bytes 393220
  7.2 75.3 %all-gather.5.cloned.1.call-start = ((), (), s32[]{:S(2)}) async-start(), calls=%async_computation.2 | async-start | bytes 5570560 | tf_op jit(solution)/shard_map/all_gather | solution.py:36
  27.2 169.7 %reduce-scatter.2.cloned.1.call-start = ((), (), s32[]{:S(2)}) async-start(), calls=%async_computation.1 | async-start | bytes 11280384 | tf_op jit(solution)/shard_map/reduce_scatter | solution.py:55
  112.9 84.0 %copy-start.3 = (u32[256]{0:T(256)S(1)}, u32[256]{0:T(256)}, u32[]{:S(2)}) copy-start(u32[256]{0:T(256)} %constant.26) | copy-start | bytes 3076
  112.9 181.3 %all-reduce.5.cloned.1.call-start = ((), (), s32[]{:S(2)}) async-start(), calls=%async_computation.3 | async-start | bytes 1327104
Sparse Core Ops, SparseCore 0:
  27.4 47.6 all-gather.4
  113.0 83.8 reduce-scatter.1
  200.2 93.9 all-reduce.4

commit v2 on v1

--- a/solution.py
+++ b/solution.py
@@ -53,9 +53,9 @@
         axis=2,
     )
     payload = lax.psum_scatter(payload, "dp", scatter_dimension=0, tiled=True)
-    payload = lax.psum_scatter(payload.reshape(n_group, -1), "group", scatter_dimension=0, tiled=True)
-    weight_grad = payload[0, :block].reshape(shard_rows, kv_width)
-    gain_grad = payload[0, block:block + shard_rows]
+    payload = lax.all_to_all(payload.reshape(n_group, -1), "group", 0, 0, tiled=True).sum(0)
+    weight_grad = payload[:block].reshape(shard_rows, kv_width)
+    gain_grad = payload[block:block + shard_rows]
     return (values, weight_grad, gain_grad)
 
 

time: 308 us -> 227 us (0.74)
  waiting for transfers between devices: 177 us -> 91.4 us
  starting transfers between devices: 0.12 us -> 6.59 us
    unnamed x4 -> x2, waiting for transfers between devices: 92.6 us -> 0.03 us
    all_to_all x0 -> x1, waiting for transfers between devices: none -> 7.21 us  [body(): lax.all_to_all(payload.reshape(n_group, -1), 'group', 0, 0, tiled=True)]
    all_to_all x0 -> x1, starting transfers between devices: none -> 6.51 us  [body(): lax.all_to_all(payload.reshape(n_group, -1), 'group', 0, 0, tiled=True)]
  transfers between devices with their start and end apart: 3 -> 3, of which waited for: 2 -> 2; matrix products, arithmetic and copies ran while one was open for 8% -> 11% of each run, Pallas kernels for 0% -> 0%
where the time goes in v2:
time: 227 us; the launch traced here: 226 us
  waiting for transfers between devices  91.4 us (40%)
  blocking collectives  50.5 us (22%)
  local copies, waits for them, and re-layouts  34.4 us (15%)
  between operations  18.1 us (8%)
  matrix products  14 us (6%)
  other arithmetic  10.9 us (5%)
  starting transfers between devices  6.59 us (3%)
    reduce_scatter x1, waiting for transfers between devices, body(): payload = lax.psum_scatter(payload, 'dp', scatter_dimension=0, tiled=True)  84.2 us
    psum x1, blocking collectives, body(): lax.psum((jnp.sum(scores, axis=1, keepdims=True), jnp.sum(scores * scores...  31.4 us
    all_gather x1, blocking collectives, body(): part = lax.all_gather(value_weight[None], 'group', axis=0, tiled=True)  19.2 us
    reshape x1, local copies, waits for them, and re-layouts, body(): grad_part.reshape(n_dp, n_group, block)  12.5 us
    reshape x1, local copies, waits for them, and re-layouts, body(): lax.all_gather(part[None], 'dp', axis=0, tiled=True)  8.97 us
    concatenate x1, other arithmetic, body(): jnp.concatenate([grad_part.reshape(n_dp, n_group, block), jnp.pad(gain_te...  8.76 us
    all_gather x1, local copies, waits for them, and re-layouts, body(): lax.all_gather(part[None], 'dp', axis=0, tiled=True)  8.16 us
    all_to_all x1, waiting for transfers between devices, body(): lax.all_to_all(payload.reshape(n_group, -1), 'group', 0, 0, tiled=True)  7.21 us
  transfers between devices with their start and end apart: 3, of which 2 were waited for; matrix products, arithmetic and copies ran while one was open for 11% of the time, Pallas kernels for 0%

profile of v2, /device:TPU:97, one launch (start us, length us, event | category | flops | bytes accessed | tf_op | source)
XLA Modules:
  0.0 225.9 jit_solution(7207550653933843299)
XLA Ops:
  7.2 0.0 copy-start
  7.2 0.0 copy-start.1
  7.2 0.0 copy-start.2
  7.2 0.0 all-gather.5.cloned.1.call-start
  7.2 19.2 %all-gather.2 = bf16[16,20,512]{2,1,0:T(8,128)(2,1)S(1)} all-gather(bf16[1,20,512]{2,1,0:T(8,128)(2,1)} %bitcast.30), channel_id=2, replica_groups=mesh['dp'=16,'group'=16] {'group'}, dimensions={0}, use_global_device_ids=true | all-gather | bytes 348160 | tf_op jit(solution)/shard_map/all_gather | solution.py:35
  26.4 0.8 copy.16
  27.2 0.0 all-gather.5.cloned.1.call-update
  27.2 0.0 reduce-scatter.2.cloned.1.call-start
  27.9 31.4 %all-reduce.1 = (f32[1,1]{1,0:T(1,128)}, f32[1,1]{1,0:T(1,128)}) all-reduce(f32[1,1]{1,0:T(1,128)S(6)} %convert_element_type.48, f32[1,1]{1,0:T(1,128)S(6)} %mul.53), channel_id=1, replica_groups=mesh['dp'=16,'group'=16] {'group'}, use_global_device_ids=true, to_apply=%region_1.0 | all-reduce | flops 2 | bytes 16 | tf_op jit(solution)/shard_map/psum | solution.py:16
  62.7 1.7 fusion.2
  64.4 0.0 copy-done
  64.4 0.0 copy-done.1
  64.4 0.0 copy-done.2
  64.4 5.6 %fusion.8 = f32[5120,512]{1,0:T(8,128)} fusion(bf16[1,1,128,5120]{3,2,1,0:T(8,128)(2,1)S(1)} %copy-done, f32[5120]{0:T(1024)S(1)} %copy-done.2, f32[128]{0:T(128)S(1)} %get-tuple-element.6, bf16[1,1,128,512]{3,2,1,0:T(8,128)(2,1)S(1)} %copy-done.1, f32[128]{0:T(128)S(1)} %get-tuple-element.5), kind=kOutput, calls=%fused_computation.14 | convolution fusion | flops 673906688 | bytes 11949056 | tf_op jit(solution)/shard_map/dot_general | solution.py:43
  70.0 12.5 %reshape.102 = f32[16,16,10240]{2,1,0:T(8,128)} reshape(f32[5120,512]{1,0:T(8,128)} %fusion.8) | data formatting | bytes 20971520 | tf_op jit(solution)/shard_map/reshape | solution.py:50
  82.5 0.0 all-gather.5.cloned.1.call-done
  82.5 8.2 %copy.17 = bf16[256,20,512]{2,1,0:T(8,128)(2,1)} copy(bf16[256,20,512]{2,0,1:T(8,128)(2,1)} %all-gather.5.cloned.1.call-done) | data formatting | bytes 10485760 | tf_op jit(solution)/shard_map/all_gather | solution.py:36
  90.7 9.0 %reshape.100 = bf16[5120,512]{1,0:T(8,128)(2,1)} reshape(bf16[256,20,512]{2,1,0:T(8,128)(2,1)} %copy.17) | data formatting | bytes 10485760 | tf_op jit(solution)/shard_map/reshape | solution.py:36
  99.6 4.3 %fusion.5 = f32[5120]{0:T(1024)S(1)} fusion(bf16[1,1,128,5120]{3,2,1,0:T(8,128)(2,1)S(1)} %copy-done, bf16[5120,512]{1,0:T(8,128)(2,1)} %reshape.100, f32[128]{0:T(128)S(1)} %get-tuple-element.6, bf16[1,1,128,512]{3,2,1,0:T(8,128)(2,1)S(1)} %copy-done.1, f32[128]{0:T(128)S(1)} %get-tuple-element.5), kind=kOutput, calls=%fused_computation.10 | convolution fusion | flops 673901568 | bytes 6706176 | tf_op jit(solution)/shard_map/dot_general | solution.py:38
  104.0 0.1 reshape.103
  104.1 8.8 %select_maximum_fusion = f32[16,16,10368]{2,1,0:T(8,128)} fusion(f32[16,16,20]{2,1,0:T(8,128)S(1)} %reshape.103, f32[16,16,10240]{2,1,0:T(8,128)} %reshape.102), kind=kLoop, calls=%fused_computation | loop fusion | flops 7962624 | bytes 21123072 | tf_op jit(solution)/shard_map/concatenate | solution.py:48
  112.9 0.0 reduce-scatter.2.cloned.1.call-update
  112.9 84.2 %reduce-scatter.2.cloned.1.call-done = f32[1,16,10368]{2,1,0:T(8,128)} async-done(((f32[16,16,10368]{2,1,0:T(8,128)}), f32[1,16,10368]{2,1,0:T(8,128)}) %reduce-scatter.2.cloned.1.call-update) | async-done | bytes 663568 | tf_op jit(solution)/shard_map/reduce_scatter | solution.py:55
  197.1 2.6 %copy.18 = f32[16,1,10368]{2,1,0:T(1,128)} copy(f32[16,1,10368]{2,0,1:T(8,128)} %bitcast.29) | data formatting | bytes 1327104 | tf_op jit(solution)/shard_map/all_to_all | solution.py:56
  199.7 6.5 %all-to-all-start = ((f32[16,1,10368]{2,1,0:T(1,128)}), f32[16,1,10368]{2,1,0:T(1,128)S(1)}, u32[]{:S(2)}, u32[]{:S(2)}) async-start(f32[16,1,10368]{2,1,0:T(1,128)} %copy.18), calls=%async_computation.1 | async-start | bytes 1327104 | tf_op jit(solution)/shard_map/all_to_all | solution.py:56
  206.3 4.0 %fusion.7 = bf16[1,1,128,512]{3,2,1,0:T(8,128)(2,1)} fusion(bf16[5120,512]{1,0:T(8,128)(2,1)} %reshape.100, bf16[1,1,128,5120]{3,2,1,0:T(8,128)(2,1)S(1)} %copy-done, f32[5120]{0:T(1024)S(1)} %copy-done.2, f32[128]{0:T(128)S(1)} %get-tuple-element.6), kind=kOutput, calls=%fused_computation.13 | convolution fusion | flops 673775616 | bytes 6705664 | tf_op jit(solution)/shard_map/dot_general | solution.py:37
  210.3 7.2 %all-to-all-done = f32[16,1,10368]{2,1,0:T(1,128)S(1)} async-done(((f32[16,1,10368]{2,1,0:T(1,128)}), f32[16,1,10368]{2,1,0:T(1,128)S(1)}, u32[]{:S(2)}, u32[]{:S(2)}) %all-to-all-start) | async-done | bytes 663584 | tf_op jit(solution)/shard_map/all_to_all | solution.py:56
  217.5 0.4 reduce_sum.29
  217.9 0.5 slice.9
  218.4 0.6 reshape.104
  (2 shorter events, 0.0 us)
Async XLA Ops:
  7.2 57.2 %copy-start = (bf16[1,1,128,5120]{3,2,1,0:T(8,128)(2,1)S(1)}, bf16[1,1,128,5120]{3,2,1,0:T(8,128)(2,1)}, u32[]{:S(2)}) copy-start(bf16[1,1,128,5120]{3,2,1,0:T(8,128)(2,1)} %param.6) | copy-start | bytes 3932164
  7.2 57.2 %copy-start.1 = (bf16[1,1,128,512]{3,2,1,0:T(8,128)(2,1)S(1)}, bf16[1,1,128,512]{3,2,1,0:T(8,128)(2,1)}, u32[]{:S(2)}) copy-start(bf16[1,1,128,512]{3,2,1,0:T(8,128)(2,1)} %param.9) | copy-start | bytes 393220
  7.2 57.2 %copy-start.2 = (f32[5120]{0:T(1024)S(1)}, f32[5120]{0:T(1024)}, u32[]{:S(2)}) copy-start(f32[5120]{0:T(1024)} %param.7) | copy-start | bytes 61444
  7.2 75.3 %all-gather.5.cloned.1.call-start = ((), (), s32[]{:S(2)}) async-start(), calls=%async_computation.3 | async-start | bytes 5570560 | tf_op jit(solution)/shard_map/all_gather | solution.py:36
  27.2 169.8 %reduce-scatter.2.cloned.1.call-start = ((), (), s32[]{:S(2)}) async-start(), calls=%async_computation.2 | async-start | bytes 11280384 | tf_op jit(solution)/shard_map/reduce_scatter | solution.py:55
  199.7 17.8 %all-to-all-start = ((f32[16,1,10368]{2,1,0:T(1,128)}), f32[16,1,10368]{2,1,0:T(1,128)S(1)}, u32[]{:S(2)}, u32[]{:S(2)}) async-start(f32[16,1,10368]{2,1,0:T(1,128)} %copy.18), calls=%async_computation.1 | async-start | bytes 1327104 | tf_op jit(solution)/shard_map/all_to_all | solution.py:56
Sparse Core Ops, SparseCore 0:
  27.4 47.6 all-gather.4
  113.0 84.0 reduce-scatter.1

commit v3 on v2

--- a/solution.py
+++ b/solution.py
@@ -32,8 +32,8 @@
         token_weight.reshape(row_count, 1)
         * value_cot.reshape(row_count, kv_width).astype(jnp.float32)
     ).astype(jnp.bfloat16)
-    part = lax.all_gather(value_weight[None], "group", axis=0, tiled=True)
-    full_weight = lax.all_gather(part[None], "dp", axis=0, tiled=True).reshape(features, kv_width)
+    part = lax.all_gather(value_weight, "group", axis=0, tiled=True)
+    full_weight = lax.all_gather(part, "dp", axis=0, tiled=True)
     projected = jnp.dot(normed, full_weight, preferred_element_type=jnp.float32)
     back = lax.dot_general(
         scaled_cot, full_weight, (((1,), (1,)), ((), ())), preferred_element_type=jnp.float32
@@ -43,19 +43,14 @@
     grad_part = lax.dot_general(
         normed, scaled_cot, (((0,), (0,)), ((), ())), preferred_element_type=jnp.float32
     )
-    block = shard_rows * kv_width
-    pad = (-shard_rows) % 128
-    payload = jnp.concatenate(
-        [
-            grad_part.reshape(n_dp, n_group, block),
-            jnp.pad(gain_term.reshape(n_dp, n_group, shard_rows), ((0, 0), (0, 0), (0, pad))),
-        ],
-        axis=2,
+    grad_part = lax.psum_scatter(
+        grad_part.reshape(n_dp, features // n_dp, kv_width), "dp", scatter_dimension=0, tiled=True
     )
-    payload = lax.psum_scatter(payload, "dp", scatter_dimension=0, tiled=True)
-    payload = lax.all_to_all(payload.reshape(n_group, -1), "group", 0, 0, tiled=True).sum(0)
-    weight_grad = payload[:block].reshape(shard_rows, kv_width)
-    gain_grad = payload[block:block + shard_rows]
+    grad_part = grad_part.reshape(n_group, shard_rows, kv_width)
+    weight_grad = lax.all_to_all(grad_part, "group", 0, 0, tiled=True).sum(0)
+    gain_part = lax.all_to_all(gain_term.reshape(n_dp, features // n_dp), "dp", 0, 0, tiled=True)
+    gain_part = gain_part.sum(0).reshape(n_group, shard_rows)
+    gain_grad = lax.all_to_all(gain_part, "group", 0, 0, tiled=True).sum(0)
     return (values, weight_grad, gain_grad)
 
 

time: 227 us -> 187 us (0.82)
  waiting for transfers between devices: 91.4 us -> 60.5 us
  local copies, waits for them, and re-layouts: 34.4 us -> 5.42 us
  blocking collectives: 50.5 us -> 73.6 us
  other arithmetic: 10.9 us -> 4.4 us
  starting transfers between devices: 6.59 us -> 10.1 us
    reduce_scatter x1, waiting for transfers between devices: 84.2 us -> 50.7 us  [body(): lax.psum_scatter(grad_part.reshape(n_dp, features // n_dp, kv_width), 'dp...]
    all_to_all x0 -> x1, blocking collectives: none -> 23.1 us  [body(): lax.all_to_all(gain_term.reshape(n_dp, features // n_dp), 'dp', 0, 0, til...]
    reshape x4 -> x1, local copies, waits for them, and re-layouts: 22.2 us -> 2.03 us  [body(): grad_part = grad_part.reshape(n_group, shard_rows, kv_width)]
    all_gather x2 -> x0, local copies, waits for them, and re-layouts: 8.99 us -> none  [the longest x1 8.16 us: body(): lax.all_gather(part[None], 'dp', axis=0, tiled=True)]
    concatenate x1 -> x0, other arithmetic: 8.76 us -> none  [body(): jnp.concatenate([grad_part.reshape(n_dp, n_group, block), jnp.pad(gain_te...]
    all_to_all x1 -> x2, starting transfers between devices: 6.51 us -> 9.97 us  [the longest x1 6.5 us: body(): weight_grad = lax.all_to_all(grad_part, 'group', 0, 0, tiled=True).sum(0)]
    all_to_all x1 -> x2, waiting for transfers between devices: 7.21 us -> 8.02 us  [the longest x1 8.02 us: body(): weight_grad = lax.all_to_all(grad_part, 'group', 0, 0, tiled=True).sum(0)]
  transfers between devices with their start and end apart: 3 -> 4, of which waited for: 2 -> 3; matrix products, arithmetic and copies ran while one was open for 11% -> 12% of each run, Pallas kernels for 0% -> 0%
where the time goes in v3:
time: 187 us; the launch traced here: 186 us
  blocking collectives  73.6 us (39%)
  waiting for transfers between devices  60.5 us (32%)
  between operations  18.1 us (10%)
  matrix products  13.9 us (7%)
  starting transfers between devices  10.1 us (5%)
  local copies, waits for them, and re-layouts  5.42 us (3%)
  other arithmetic  4.4 us (2%)
    reduce_scatter x1, waiting for transfers between devices, body(): lax.psum_scatter(grad_part.reshape(n_dp, features // n_dp, kv_width), 'dp...  50.7 us
    psum x1, blocking collectives, body(): lax.psum((jnp.sum(scores, axis=1, keepdims=True), jnp.sum(scores * scores...  31.4 us
    all_to_all x1, blocking collectives, body(): lax.all_to_all(gain_term.reshape(n_dp, features // n_dp), 'dp', 0, 0, til...  23.1 us
    all_gather x1, blocking collectives, body(): part = lax.all_gather(value_weight, 'group', axis=0, tiled=True)  19.2 us
    all_to_all x1, waiting for transfers between devices, body(): weight_grad = lax.all_to_all(grad_part, 'group', 0, 0, tiled=True).sum(0)  8.02 us
    all_to_all x1, starting transfers between devices, body(): weight_grad = lax.all_to_all(grad_part, 'group', 0, 0, tiled=True).sum(0)  6.5 us
    dot_general x1, matrix products, body(): lax.dot_general(normed, scaled_cot, (((0,), (0,)), ((), ())), preferred_e...  5.57 us
    dot_general x1, matrix products, body(): lax.dot_general(scaled_cot, full_weight, (((1,), (1,)), ((), ())), prefer...  4.32 us
  transfers between devices with their start and end apart: 4, of which 3 were waited for; matrix products, arithmetic and copies ran while one was open for 12% of the time, Pallas kernels for 0%

profile of v3, /device:TPU:97, one launch (start us, length us, event | category | flops | bytes accessed | tf_op | source)
XLA Modules:
  0.0 186.0 jit_solution(5950519298025056290)
XLA Ops:
  7.2 0.0 copy-start
  7.2 0.0 copy-start.2
  7.2 0.0 all-gather.3.cloned.1.call-start
  7.2 19.2 %all-gather = bf16[16,20,512]{2,1,0:T(8,128)(2,1)S(1)} all-gather(bf16[1,20,512]{2,1,0:T(8,128)(2,1)} %bitcast.35), channel_id=1, replica_groups=mesh['dp'=16,'group'=16] {'group'}, dimensions={0}, use_global_device_ids=true | all-gather | bytes 348160 | tf_op jit(solution)/shard_map/all_gather | solution.py:35
  26.4 0.8 reshape.69
  27.2 0.0 all-gather.3.cloned.1.call-update
  27.2 0.0 reduce-scatter.2.cloned.1.call-start
  27.9 31.4 %all-reduce = (f32[1,1]{1,0:T(1,128)}, f32[1,1]{1,0:T(1,128)}) all-reduce(f32[1,1]{1,0:T(1,128)S(6)} %convert_element_type.41, f32[1,1]{1,0:T(1,128)S(6)} %mul.48), channel_id=1, replica_groups=mesh['dp'=16,'group'=16] {'group'}, use_global_device_ids=true, to_apply=%region_1.0 | all-reduce | flops 2 | bytes 16 | tf_op jit(solution)/shard_map/psum | solution.py:16
  62.6 1.7 fusion.2
  64.3 0.0 copy-done
  64.3 0.0 copy-done.2
  64.4 0.0 copy-start.1
  64.4 1.5 fusion.5
  65.8 1.8 copy.13
  67.6 0.0 copy-done.1
  67.6 5.6 %fusion.12 = f32[16,320,512]{2,1,0:T(8,128)} fusion(bf16[16,320,128]{2,1,0:T(8,128)(2,1)S(1)} %bitcast.33, bf16[1,1,128,512]{3,2,1,0:T(8,128)(2,1)S(1)} %copy-done.1, f32[128]{0:T(128)S(1)} %get-tuple-element.5), kind=kOutput, calls=%fused_computation.16 | convolution fusion | flops 671285248 | bytes 11928064 | tf_op jit(solution)/shard_map/dot_general | solution.py:43
  73.2 0.0 reduce-scatter.2.cloned.1.call-update
  73.2 1.8 all-gather.3.cloned.1.call-done
  75.0 4.3 %fusion.3 = f32[5120]{0:T(1024)S(1)} fusion(bf16[5120,512]{1,0:T(8,128)(2,1)} %all-gather.3.cloned.1.call-done, bf16[1,1,128,5120]{3,2,1,0:T(8,128)(2,1)S(1)} %copy-done, f32[128]{0:T(128)S(1)} %get-tuple-element.6, bf16[1,1,128,512]{3,2,1,0:T(8,128)(2,1)S(1)} %copy-done.1, f32[128]{0:T(128)S(1)} %get-tuple-element.5), kind=kOutput, calls=%fused_computation.6 | convolution fusion | flops 673901568 | bytes 6706176 | tf_op jit(solution)/shard_map/dot_general | solution.py:38
  79.3 0.1 all_to_all.16
  79.4 23.1 %all_to_all.23 = f32[16,1,320]{2,1,0:T(1,128)S(1)} all-to-all(f32[16,1,320]{2,1,0:T(1,128)S(1)} %all_to_all.16), channel_id=1, replica_groups=mesh['dp'=16,'group'=16] {'dp'}, dimensions={0} | all-to-all | bytes 40960 | tf_op jit(solution)/shard_map/all_to_all | solution.py:51
  102.5 0.7 all_to_all.18
  103.2 3.5 %all-to-all-start.2 = ((f32[16,1,20]{2,1,0:T(1,128)}), f32[16,1,20]{2,1,0:T(1,128)S(1)}, u32[]{:S(2)}, u32[]{:S(2)}) async-start(f32[16,1,20]{2,1,0:T(1,128)} %all_to_all.18), calls=%async_computation.3 | async-start | bytes 16384 | tf_op jit(solution)/shard_map/all_to_all | solution.py:53
  106.7 50.7 %reduce-scatter.2.cloned.1.call-done = f32[1,320,512]{2,1,0:T(8,128)} async-done(((f32[16,320,512]{2,1,0:T(8,128)}), f32[1,320,512]{2,1,0:T(8,128)}) %reduce-scatter.2.cloned.1.call-update) | async-done | bytes 655376 | tf_op jit(solution)/shard_map/reduce_scatter | solution.py:46
  157.4 2.0 %reshape.65 = f32[16,20,512]{2,1,0:T(8,128)} reshape(f32[1,320,512]{2,1,0:T(8,128)} %reduce-scatter.2.cloned.1.call-done) | data formatting | bytes 1310720 | tf_op jit(solution)/shard_map/reshape | solution.py:49
  159.4 0.0 all-to-all-done.2
  159.4 6.5 %all-to-all-start = ((f32[16,20,512]{2,1,0:T(8,128)}), f32[16,20,512]{2,1,0:T(8,128)S(1)}, u32[]{:S(2)}, u32[]{:S(2)}) async-start(f32[16,20,512]{2,1,0:T(8,128)} %reshape.65), calls=%async_computation.1 | async-start | bytes 1572864 | tf_op jit(solution)/shard_map/all_to_all | solution.py:50
  165.9 4.0 %fusion.4 = bf16[1,1,128,512]{3,2,1,0:T(8,128)(2,1)} fusion(bf16[5120,512]{1,0:T(8,128)(2,1)} %all-gather.3.cloned.1.call-done, bf16[1,1,128,5120]{3,2,1,0:T(8,128)(2,1)S(1)} %copy-done, f32[5120]{0:T(1024)S(1)} %copy-done.2, f32[128]{0:T(128)S(1)} %get-tuple-element.6), kind=kOutput, calls=%fused_computation.8 | convolution fusion | flops 673775616 | bytes 6705664 | tf_op jit(solution)/shard_map/dot_general | solution.py:37
  169.9 0.5 reduce_sum.57
  170.5 8.0 %all-to-all-done = f32[16,20,512]{2,1,0:T(8,128)S(1)} async-done(((f32[16,20,512]{2,1,0:T(8,128)}), f32[16,20,512]{2,1,0:T(8,128)S(1)}, u32[]{:S(2)}, u32[]{:S(2)}) %all-to-all-start) | async-done | bytes 655392 | tf_op jit(solution)/shard_map/all_to_all | solution.py:50
  178.5 0.7 reduce_sum.44
  (2 shorter events, 0.0 us)
Async XLA Ops:
  7.2 57.2 %copy-start = (bf16[1,1,128,5120]{3,2,1,0:T(8,128)(2,1)S(1)}, bf16[1,1,128,5120]{3,2,1,0:T(8,128)(2,1)}, u32[]{:S(2)}) copy-start(bf16[1,1,128,5120]{3,2,1,0:T(8,128)(2,1)} %param.6) | copy-start | bytes 3932164
  7.2 57.2 %copy-start.2 = (f32[5120]{0:T(1024)S(1)}, f32[5120]{0:T(1024)}, u32[]{:S(2)}) copy-start(f32[5120]{0:T(1024)} %param.7) | copy-start | bytes 61444
  7.2 67.8 %all-gather.3.cloned.1.call-start = ((), (), s32[]{:S(2)}) async-start(), calls=%async_computation.4 | async-start | bytes 5570560 | tf_op jit(solution)/shard_map/all_gather | solution.py:36
  27.2 130.2 %reduce-scatter.2.cloned.1.call-start = ((), (), s32[]{:S(2)}) async-start(), calls=%async_computation.5 | async-start | bytes 11141120 | tf_op jit(solution)/shard_map/reduce_scatter | solution.py:46
  64.4 3.3 %copy-start.1 = (bf16[1,1,128,512]{3,2,1,0:T(8,128)(2,1)S(1)}, bf16[1,1,128,512]{3,2,1,0:T(8,128)(2,1)}, u32[]{:S(2)}) copy-start(bf16[1,1,128,512]{3,2,1,0:T(8,128)(2,1)} %param.9) | copy-start | bytes 393220
  103.2 56.2 %all-to-all-start.2 = ((f32[16,1,20]{2,1,0:T(1,128)}), f32[16,1,20]{2,1,0:T(1,128)S(1)}, u32[]{:S(2)}, u32[]{:S(2)}) async-start(f32[16,1,20]{2,1,0:T(1,128)} %all_to_all.18), calls=%async_computation.3 | async-start | bytes 16384 | tf_op jit(solution)/shard_map/all_to_all | solution.py:53
  159.4 19.1 %all-to-all-start = ((f32[16,20,512]{2,1,0:T(8,128)}), f32[16,20,512]{2,1,0:T(8,128)S(1)}, u32[]{:S(2)}, u32[]{:S(2)}) async-start(f32[16,20,512]{2,1,0:T(8,128)} %reshape.65), calls=%async_computation.1 | async-start | bytes 1572864 | tf_op jit(solution)/shard_map/all_to_all | solution.py:50
Sparse Core Ops, SparseCore 0:
  27.3 47.6 all-gather.2
  77.6 79.7 reduce-scatter.1

commit v4 on v3

--- a/solution.py
+++ b/solution.py
@@ -13,10 +13,11 @@
     group_count = answers * n_group
     shard_rows = value_weight.shape[0]
     scores = rewards.astype(jnp.float32)
-    reward_sum, square_sum = lax.psum(
-        (jnp.sum(scores, axis=1, keepdims=True), jnp.sum(scores * scores, axis=1, keepdims=True)),
-        "group",
+    peer_scores = lax.all_to_all(
+        jnp.broadcast_to(scores.reshape(1, -1), (n_group, scores.size)), "group", 0, 0, tiled=True
     )
+    reward_sum = jnp.sum(peer_scores).reshape(1, 1)
+    square_sum = jnp.sum(peer_scores * peer_scores).reshape(1, 1)
     centre = reward_sum / group_count
     spread = square_sum / group_count - centre * centre
     advantage = (scores - centre) / jnp.maximum(jnp.sqrt(spread), 1.0)

time: 187 us -> 181 us (0.968)
  blocking collectives: 73.6 us -> 29 us
  waiting for transfers between devices: 60.5 us -> 89.8 us
  starting transfers between devices: 10.1 us -> 17.5 us
    psum x1 -> x0, blocking collectives: 31.4 us -> none  [body(): lax.psum((jnp.sum(scores, axis=1, keepdims=True), jnp.sum(scores * scores...]
    all_gather x1, waiting for transfers between devices: 1.78 us -> 22.6 us  [body(): full_weight = lax.all_gather(part, 'dp', axis=0, tiled=True)]
    all_to_all x1, blocking collectives: 23.1 us -> 9.82 us  [body(): lax.all_to_all(gain_term.reshape(n_dp, features // n_dp), 'dp', 0, 0, til...]
    all_to_all x0 -> x1, starting transfers between devices: none -> 4.67 us  [body(): lax.all_to_all(jnp.broadcast_to(scores.reshape(1, -1), (n_group, scores.s...]
    reduce_scatter x1, waiting for transfers between devices: 50.7 us -> 55.1 us  [body(): lax.psum_scatter(grad_part.reshape(n_dp, features // n_dp, kv_width), 'dp...]
    all_to_all x0 -> x1, waiting for transfers between devices: none -> 4.01 us  [body(): lax.all_to_all(jnp.broadcast_to(scores.reshape(1, -1), (n_group, scores.s...]
    all_to_all x1, starting transfers between devices: 3.47 us -> 6.39 us  [body(): gain_grad = lax.all_to_all(gain_part, 'group', 0, 0, tiled=True).sum(0)]
  transfers between devices with their start and end apart: 4 -> 5, of which waited for: 3 -> 4; matrix products, arithmetic and copies ran while one was open for 12% -> 13% of each run, Pallas kernels for 0% -> 0%
where the time goes in v4:
time: 181 us; the launch traced here: 180 us
  waiting for transfers between devices  89.8 us (50%)
  blocking collectives  29 us (16%)
  between operations  18.1 us (10%)
  starting transfers between devices  17.5 us (10%)
  matrix products  13.9 us (8%)
  local copies, waits for them, and re-layouts  6.07 us (3%)
  other arithmetic  5.58 us (3%)
    reduce_scatter x1, waiting for transfers between devices, body(): lax.psum_scatter(grad_part.reshape(n_dp, features // n_dp, kv_width), 'dp...  55.1 us
    all_gather x1, waiting for transfers between devices, body(): full_weight = lax.all_gather(part, 'dp', axis=0, tiled=True)  22.6 us
    all_gather x1, blocking collectives, body(): part = lax.all_gather(value_weight, 'group', axis=0, tiled=True)  19.2 us
    all_to_all x1, blocking collectives, body(): lax.all_to_all(gain_term.reshape(n_dp, features // n_dp), 'dp', 0, 0, til...  9.82 us
    all_to_all x1, waiting for transfers between devices, body(): weight_grad = lax.all_to_all(grad_part, 'group', 0, 0, tiled=True).sum(0)  8.05 us
    all_to_all x1, starting transfers between devices, body(): gain_grad = lax.all_to_all(gain_part, 'group', 0, 0, tiled=True).sum(0)  6.39 us
    all_to_all x1, starting transfers between devices, body(): weight_grad = lax.all_to_all(grad_part, 'group', 0, 0, tiled=True).sum(0)  6.36 us
    dot_general x1, matrix products, body(): lax.dot_general(normed, scaled_cot, (((0,), (0,)), ((), ())), preferred_e...  5.57 us
  transfers between devices with their start and end apart: 5, of which 4 were waited for; matrix products, arithmetic and copies ran while one was open for 13% of the time, Pallas kernels for 0%

profile of v4, /device:TPU:97, one launch (start us, length us, event | category | flops | bytes accessed | tf_op | source)
XLA Modules:
  0.0 180.0 jit_solution(2975889256579668342)
XLA Ops:
  7.2 0.0 copy-start
  7.2 0.0 copy-start.2
  7.2 0.0 all-gather.3.cloned.1.call-start
  7.2 19.2 %all-gather = bf16[16,20,512]{2,1,0:T(8,128)(2,1)S(1)} all-gather(bf16[1,20,512]{2,1,0:T(8,128)(2,1)} %bitcast.38), channel_id=1, replica_groups=mesh['dp'=16,'group'=16] {'group'}, dimensions={0}, use_global_device_ids=true | all-gather | bytes 348160 | tf_op jit(solution)/shard_map/all_gather | solution.py:36
  26.4 0.8 reshape.96
  27.2 0.0 all-gather.3.cloned.1.call-update
  27.8 0.6 broadcast_in_dim.27
  28.5 4.7 %all-to-all-start = ((f32[16,1,1]{2,1,0:T(1,128)}), f32[16,1,1]{2,1,0:T(1,128)S(1)}, u32[]{:S(2)}, u32[]{:S(2)}) async-start(f32[16,1,1]{2,1,0:T(1,128)} %broadcast_in_dim.27), calls=%async_computation | async-start | bytes 16384 | tf_op jit(solution)/shard_map/all_to_all | solution.py:16
  33.1 0.0 reduce-scatter.2.cloned.1.call-start
  33.8 1.7 fusion.2
  35.5 4.0 %all-to-all-done = f32[16,1,1]{2,1,0:T(1,128)S(1)} async-done(((f32[16,1,1]{2,1,0:T(1,128)}), f32[16,1,1]{2,1,0:T(1,128)S(1)}, u32[]{:S(2)}, u32[]{:S(2)}) %all-to-all-start) | async-done | bytes 96 | tf_op jit(solution)/shard_map/all_to_all | solution.py:16
  39.5 0.6 reduce_sum.64
  42.1 0.1 copy.19
  42.1 0.6 multiply_reduce_fusion
  43.5 0.0 copy-done
  43.5 0.0 copy-done.2
  43.5 0.0 copy-start.1
  43.5 1.5 fusion.5
  45.0 1.8 copy.18
  46.8 0.0 copy-done.1
  46.8 5.6 %fusion.12 = f32[16,320,512]{2,1,0:T(8,128)} fusion(bf16[16,320,128]{2,1,0:T(8,128)(2,1)S(1)} %bitcast.36, bf16[1,1,128,512]{3,2,1,0:T(8,128)(2,1)S(1)} %copy-done.1, f32[128]{0:T(128)S(1)} %get-tuple-element.3), kind=kOutput, calls=%fused_computation.16 | convolution fusion | flops 671285248 | bytes 11928064 | tf_op jit(solution)/shard_map/dot_general | solution.py:44
  52.3 0.0 reduce-scatter.2.cloned.1.call-update
  52.4 22.6 %all-gather.3.cloned.1.call-done = bf16[5120,512]{1,0:T(8,128)(2,1)} async-done(((bf16[320,512]{1,0:T(8,128)(2,1)}), bf16[5120,512]{1,0:T(8,128)(2,1)}) %all-gather.3.cloned.1.call-update) | async-done | bytes 5242896 | tf_op jit(solution)/shard_map/all_gather | solution.py:37
  75.0 4.3 %fusion.3 = f32[5120]{0:T(1024)S(1)} fusion(bf16[5120,512]{1,0:T(8,128)(2,1)} %all-gather.3.cloned.1.call-done, bf16[1,1,128,5120]{3,2,1,0:T(8,128)(2,1)S(1)} %copy-done, f32[128]{0:T(128)S(1)} %get-tuple-element.4, bf16[1,1,128,512]{3,2,1,0:T(8,128)(2,1)S(1)} %copy-done.1, f32[128]{0:T(128)S(1)} %get-tuple-element.3), kind=kOutput, calls=%fused_computation.6 | convolution fusion | flops 673901568 | bytes 6706176 | tf_op jit(solution)/shard_map/dot_general | solution.py:39
  79.3 0.1 all_to_all.21
  79.4 9.8 %all_to_all.29 = f32[16,1,320]{2,1,0:T(1,128)S(1)} all-to-all(f32[16,1,320]{2,1,0:T(1,128)S(1)} %all_to_all.21), channel_id=1, replica_groups=mesh['dp'=16,'group'=16] {'dp'}, dimensions={0} | all-to-all | bytes 40960 | tf_op jit(solution)/shard_map/all_to_all | solution.py:52
  89.3 0.7 all_to_all.23
  90.0 6.4 %all-to-all-start.3 = ((f32[16,1,20]{2,1,0:T(1,128)}), f32[16,1,20]{2,1,0:T(1,128)S(1)}, u32[]{:S(2)}, u32[]{:S(2)}) async-start(f32[16,1,20]{2,1,0:T(1,128)} %all_to_all.23), calls=%async_computation.4 | async-start | bytes 16384 | tf_op jit(solution)/shard_map/all_to_all | solution.py:54
  96.4 55.1 %reduce-scatter.2.cloned.1.call-done = f32[1,320,512]{2,1,0:T(8,128)} async-done(((f32[16,320,512]{2,1,0:T(8,128)}), f32[1,320,512]{2,1,0:T(8,128)}) %reduce-scatter.2.cloned.1.call-update) | async-done | bytes 655376 | tf_op jit(solution)/shard_map/reduce_scatter | solution.py:47
  151.4 2.0 %reshape.90 = f32[16,20,512]{2,1,0:T(8,128)} reshape(f32[1,320,512]{2,1,0:T(8,128)} %reduce-scatter.2.cloned.1.call-done) | data formatting | bytes 1310720 | tf_op jit(solution)/shard_map/reshape | solution.py:50
  153.5 0.0 all-to-all-done.3
  153.5 6.4 %all-to-all-start.1 = ((f32[16,20,512]{2,1,0:T(8,128)}), f32[16,20,512]{2,1,0:T(8,128)S(1)}, u32[]{:S(2)}, u32[]{:S(2)}) async-start(f32[16,20,512]{2,1,0:T(8,128)} %reshape.90), calls=%async_computation.2 | async-start | bytes 1572864 | tf_op jit(solution)/shard_map/all_to_all | solution.py:51
  159.8 4.0 %fusion.4 = bf16[1,1,128,512]{3,2,1,0:T(8,128)(2,1)} fusion(bf16[5120,512]{1,0:T(8,128)(2,1)} %all-gather.3.cloned.1.call-done, bf16[1,1,128,5120]{3,2,1,0:T(8,128)(2,1)S(1)} %copy-done, f32[5120]{0:T(1024)S(1)} %copy-done.2, f32[128]{0:T(128)S(1)} %get-tuple-element.4), kind=kOutput, calls=%fused_computation.8 | convolution fusion | flops 673775616 | bytes 6705664 | tf_op jit(solution)/shard_map/dot_general | solution.py:38
  163.9 0.5 reduce_sum.69
  164.4 8.0 %all-to-all-done.1 = f32[16,20,512]{2,1,0:T(8,128)S(1)} async-done(((f32[16,20,512]{2,1,0:T(8,128)}), f32[16,20,512]{2,1,0:T(8,128)S(1)}, u32[]{:S(2)}, u32[]{:S(2)}) %all-to-all-start.1) | async-done | bytes 655392 | tf_op jit(solution)/shard_map/all_to_all | solution.py:51
  172.4 0.7 reduce_sum.66
  (2 shorter events, 0.0 us)
Async XLA Ops:
  7.2 36.3 %copy-start = (bf16[1,1,128,5120]{3,2,1,0:T(8,128)(2,1)S(1)}, bf16[1,1,128,5120]{3,2,1,0:T(8,128)(2,1)}, u32[]{:S(2)}) copy-start(bf16[1,1,128,5120]{3,2,1,0:T(8,128)(2,1)} %param.6) | copy-start | bytes 3932164
  7.2 36.3 %copy-start.2 = (f32[5120]{0:T(1024)S(1)}, f32[5120]{0:T(1024)}, u32[]{:S(2)}) copy-start(f32[5120]{0:T(1024)} %param.7) | copy-start | bytes 61444
  7.2 67.8 %all-gather.3.cloned.1.call-start = ((), (), s32[]{:S(2)}) async-start(), calls=%async_computation.5 | async-start | bytes 5570560 | tf_op jit(solution)/shard_map/all_gather | solution.py:37
  28.5 11.0 %all-to-all-start = ((f32[16,1,1]{2,1,0:T(1,128)}), f32[16,1,1]{2,1,0:T(1,128)S(1)}, u32[]{:S(2)}, u32[]{:S(2)}) async-start(f32[16,1,1]{2,1,0:T(1,128)} %broadcast_in_dim.27), calls=%async_computation | async-start | bytes 16384 | tf_op jit(solution)/shard_map/all_to_all | solution.py:16
  33.1 118.3 %reduce-scatter.2.cloned.1.call-start = ((), (), s32[]{:S(2)}) async-start(), calls=%async_computation.6 | async-start | bytes 11141120 | tf_op jit(solution)/shard_map/reduce_scatter | solution.py:47
  43.5 3.2 %copy-start.1 = (bf16[1,1,128,512]{3,2,1,0:T(8,128)(2,1)S(1)}, bf16[1,1,128,512]{3,2,1,0:T(8,128)(2,1)}, u32[]{:S(2)}) copy-start(bf16[1,1,128,512]{3,2,1,0:T(8,128)(2,1)} %param.9) | copy-start | bytes 393220
  90.0 63.5 %all-to-all-start.3 = ((f32[16,1,20]{2,1,0:T(1,128)}), f32[16,1,20]{2,1,0:T(1,128)S(1)}, u32[]{:S(2)}, u32[]{:S(2)}) async-start(f32[16,1,20]{2,1,0:T(1,128)} %all_to_all.23), calls=%async_computation.4 | async-start | bytes 16384 | tf_op jit(solution)/shard_map/all_to_all | solution.py:54
  153.5 19.0 %all-to-all-start.1 = ((f32[16,20,512]{2,1,0:T(8,128)}), f32[16,20,512]{2,1,0:T(8,128)S(1)}, u32[]{:S(2)}, u32[]{:S(2)}) async-start(f32[16,20,512]{2,1,0:T(8,128)} %reshape.90), calls=%async_computation.2 | async-start | bytes 1572864 | tf_op jit(solution)/shard_map/all_to_all | solution.py:51
Sparse Core Ops, SparseCore 0:
  27.3 47.6 all-gather.2
  77.5 73.8 reduce-scatter.1

commit v5 on v4

--- a/solution.py
+++ b/solution.py
@@ -33,7 +33,9 @@
         token_weight.reshape(row_count, 1)
         * value_cot.reshape(row_count, kv_width).astype(jnp.float32)
     ).astype(jnp.bfloat16)
-    part = lax.all_gather(value_weight, "group", axis=0, tiled=True)
+    part = lax.all_to_all(
+        jnp.broadcast_to(value_weight[None], (n_group,) + value_weight.shape), "group", 0, 0, tiled=True
+    ).reshape(n_group * shard_rows, kv_width)
     full_weight = lax.all_gather(part, "dp", axis=0, tiled=True)
     projected = jnp.dot(normed, full_weight, preferred_element_type=jnp.float32)
     back = lax.dot_general(

time: 181 us -> 173 us (0.956)
  blocking collectives: 29 us -> 24.7 us
  waiting for transfers between devices: 89.8 us -> 87.3 us
    all_gather x1 -> x0, blocking collectives: 19.2 us -> none  [body(): part = lax.all_gather(value_weight, 'group', axis=0, tiled=True)]
    all_to_all x0 -> x1, blocking collectives: none -> 14.8 us  [body(): lax.all_to_all(jnp.broadcast_to(value_weight[None], (n_group,) + value_we...]
    all_gather x1, waiting for transfers between devices: 22.6 us -> 18.6 us  [body(): full_weight = lax.all_gather(part, 'dp', axis=0, tiled=True)]
where the time goes in v5:
time: 173 us; the launch traced here: 172 us
  waiting for transfers between devices  87.3 us (50%)
  blocking collectives  24.7 us (14%)
  between operations  18.1 us (10%)
  starting transfers between devices  16.8 us (10%)
  matrix products  13.9 us (8%)
  local copies, waits for them, and re-layouts  6.93 us (4%)
  other arithmetic  4.26 us (2%)
    reduce_scatter x1, waiting for transfers between devices, body(): lax.psum_scatter(grad_part.reshape(n_dp, features // n_dp, kv_width), 'dp...  55.3 us
    all_gather x1, waiting for transfers between devices, body(): full_weight = lax.all_gather(part, 'dp', axis=0, tiled=True)  18.6 us
    all_to_all x1, blocking collectives, body(): lax.all_to_all(jnp.broadcast_to(value_weight[None], (n_group,) + value_we...  14.8 us
    all_to_all x1, blocking collectives, body(): lax.all_to_all(gain_term.reshape(n_dp, features // n_dp), 'dp', 0, 0, til...  9.89 us
    all_to_all x1, waiting for transfers between devices, body(): weight_grad = lax.all_to_all(grad_part, 'group', 0, 0, tiled=True).sum(0)  8.05 us
    all_to_all x1, starting transfers between devices, body(): gain_grad = lax.all_to_all(gain_part, 'group', 0, 0, tiled=True).sum(0)  6.47 us
    all_to_all x1, starting transfers between devices, body(): weight_grad = lax.all_to_all(grad_part, 'group', 0, 0, tiled=True).sum(0)  6.14 us
    dot_general x1, matrix products, body(): lax.dot_general(normed, scaled_cot, (((0,), (0,)), ((), ())), preferred_e...  5.57 us
  transfers between devices with their start and end apart: 5, of which 4 were waited for; matrix products, arithmetic and copies ran while one was open for 13% of the time, Pallas kernels for 0%

profile of v5, /device:TPU:97, one launch (start us, length us, event | category | flops | bytes accessed | tf_op | source)
XLA Modules:
  0.0 172.1 jit_solution(1051084549673686497)
XLA Ops:
  7.2 0.0 copy-start
  7.2 0.0 copy-start.2
  7.2 0.0 all-gather.2.cloned.1.call-start
  7.2 0.9 broadcast_in_dim.32
  8.1 14.8 %all_to_all.34 = bf16[16,20,512]{2,1,0:T(8,128)(2,1)S(1)} all-to-all(bf16[16,20,512]{2,1,0:T(8,128)(2,1)S(1)} %broadcast_in_dim.32), channel_id=1, replica_groups=mesh['dp'=16,'group'=16] {'group'}, dimensions={0} | all-to-all | bytes 655360 | tf_op jit(solution)/shard_map/all_to_all | solution.py:36
  22.9 0.8 reshape.93
  23.7 0.0 all-gather.2.cloned.1.call-update
  24.4 0.6 broadcast_in_dim.34
  25.0 4.1 %all-to-all-start.1 = ((f32[16,1,1]{2,1,0:T(1,128)}), f32[16,1,1]{2,1,0:T(1,128)S(1)}, u32[]{:S(2)}, u32[]{:S(2)}) async-start(f32[16,1,1]{2,1,0:T(1,128)} %broadcast_in_dim.34), calls=%async_computation.1 | async-start | bytes 16384 | tf_op jit(solution)/shard_map/all_to_all | solution.py:16
  29.1 0.0 reduce-scatter.2.cloned.1.call-start
  29.8 0.0 copy-done
  29.8 0.3 fusion.2
  30.2 5.3 %all-to-all-done.1 = f32[16,1,1]{2,1,0:T(1,128)S(1)} async-done(((f32[16,1,1]{2,1,0:T(1,128)}), f32[16,1,1]{2,1,0:T(1,128)S(1)}, u32[]{:S(2)}, u32[]{:S(2)}) %all-to-all-start.1) | async-done | bytes 96 | tf_op jit(solution)/shard_map/all_to_all | solution.py:16
  35.5 0.6 reduce_sum.64
  38.1 0.1 copy.18
  38.1 0.6 multiply_reduce_fusion
  39.5 0.0 copy-done.2
  39.5 0.0 copy-start.1
  39.5 1.5 fusion.5
  41.0 1.8 %copy.17 = bf16[5120,128]{1,0:T(8,128)(2,1)S(1)} copy(bf16[5120,128]{0,1:T(8,128)(2,1)} %fusion.5) | data formatting | bytes 2621440 | tf_op jit(solution)/shard_map/dot_general | solution.py:46
  42.7 0.0 copy-done.1
  42.8 5.6 %fusion.12 = f32[16,320,512]{2,1,0:T(8,128)} fusion(bf16[16,320,128]{2,1,0:T(8,128)(2,1)S(1)} %bitcast.35, bf16[1,1,128,512]{3,2,1,0:T(8,128)(2,1)S(1)} %copy-done.1, f32[128]{0:T(128)S(1)} %get-tuple-element.3), kind=kOutput, calls=%fused_computation.16 | convolution fusion | flops 671285248 | bytes 11928064 | tf_op jit(solution)/shard_map/dot_general | solution.py:46
  48.3 0.0 reduce-scatter.2.cloned.1.call-update
  48.4 18.6 %all-gather.2.cloned.1.call-done = bf16[5120,512]{1,0:T(8,128)(2,1)} async-done(((bf16[320,512]{1,0:T(8,128)(2,1)}), bf16[5120,512]{1,0:T(8,128)(2,1)}) %all-gather.2.cloned.1.call-update) | async-done | bytes 5242896 | tf_op jit(solution)/shard_map/all_gather | solution.py:39
  66.9 4.3 %fusion.3 = f32[5120]{0:T(1024)S(1)} fusion(bf16[5120,512]{1,0:T(8,128)(2,1)} %all-gather.2.cloned.1.call-done, bf16[1,1,128,5120]{3,2,1,0:T(8,128)(2,1)S(1)} %copy-done, f32[128]{0:T(128)S(1)} %get-tuple-element.4, bf16[1,1,128,512]{3,2,1,0:T(8,128)(2,1)S(1)} %copy-done.1, f32[128]{0:T(128)S(1)} %get-tuple-element.3), kind=kOutput, calls=%fused_computation.6 | convolution fusion | flops 673901568 | bytes 6706176 | tf_op jit(solution)/shard_map/dot_general | solution.py:41
  71.3 0.1 all_to_all.25
  71.4 9.9 %all_to_all.35 = f32[16,1,320]{2,1,0:T(1,128)S(1)} all-to-all(f32[16,1,320]{2,1,0:T(1,128)S(1)} %all_to_all.25), channel_id=1, replica_groups=mesh['dp'=16,'group'=16] {'dp'}, dimensions={0} | all-to-all | bytes 40960 | tf_op jit(solution)/shard_map/all_to_all | solution.py:54
  81.3 0.7 all_to_all.27
  82.0 6.5 %all-to-all-start.4 = ((f32[16,1,20]{2,1,0:T(1,128)}), f32[16,1,20]{2,1,0:T(1,128)S(1)}, u32[]{:S(2)}, u32[]{:S(2)}) async-start(f32[16,1,20]{2,1,0:T(1,128)} %all_to_all.27), calls=%async_computation.5 | async-start | bytes 16384 | tf_op jit(solution)/shard_map/all_to_all | solution.py:56
  88.5 55.3 %reduce-scatter.2.cloned.1.call-done = f32[1,320,512]{2,1,0:T(8,128)} async-done(((f32[16,320,512]{2,1,0:T(8,128)}), f32[1,320,512]{2,1,0:T(8,128)}) %reduce-scatter.2.cloned.1.call-update) | async-done | bytes 655376 | tf_op jit(solution)/shard_map/reduce_scatter | solution.py:49
  143.8 2.0 %reshape.95 = f32[16,20,512]{2,1,0:T(8,128)} reshape(f32[1,320,512]{2,1,0:T(8,128)} %reduce-scatter.2.cloned.1.call-done) | data formatting | bytes 1310720 | tf_op jit(solution)/shard_map/reshape | solution.py:52
  145.8 0.0 all-to-all-done.4
  145.8 6.1 %all-to-all-start.2 = ((f32[16,20,512]{2,1,0:T(8,128)}), f32[16,20,512]{2,1,0:T(8,128)S(1)}, u32[]{:S(2)}, u32[]{:S(2)}) async-start(f32[16,20,512]{2,1,0:T(8,128)} %reshape.95), calls=%async_computation.3 | async-start | bytes 1572864 | tf_op jit(solution)/shard_map/all_to_all | solution.py:53
  151.9 4.0 %fusion.4 = bf16[1,1,128,512]{3,2,1,0:T(8,128)(2,1)} fusion(bf16[5120,512]{1,0:T(8,128)(2,1)} %all-gather.2.cloned.1.call-done, bf16[1,1,128,5120]{3,2,1,0:T(8,128)(2,1)S(1)} %copy-done, f32[5120]{0:T(1024)S(1)} %copy-done.2, f32[128]{0:T(128)S(1)} %get-tuple-element.4), kind=kOutput, calls=%fused_computation.8 | convolution fusion | flops 673775616 | bytes 6705664 | tf_op jit(solution)/shard_map/dot_general | solution.py:40
  156.0 0.5 reduce_sum.69
  156.5 8.1 %all-to-all-done.2 = f32[16,20,512]{2,1,0:T(8,128)S(1)} async-done(((f32[16,20,512]{2,1,0:T(8,128)}), f32[16,20,512]{2,1,0:T(8,128)S(1)}, u32[]{:S(2)}, u32[]{:S(2)}) %all-to-all-start.2) | async-done | bytes 655392 | tf_op jit(solution)/shard_map/all_to_all | solution.py:53
  164.6 0.7 reduce_sum.66
  (2 shorter events, 0.0 us)
Async XLA Ops:
  7.2 22.7 %copy-start = (bf16[1,1,128,5120]{3,2,1,0:T(8,128)(2,1)S(1)}, bf16[1,1,128,5120]{3,2,1,0:T(8,128)(2,1)}, u32[]{:S(2)}) copy-start(bf16[1,1,128,5120]{3,2,1,0:T(8,128)(2,1)} %param.6) | copy-start | bytes 3932164
  7.2 32.3 %copy-start.2 = (f32[5120]{0:T(1024)S(1)}, f32[5120]{0:T(1024)}, u32[]{:S(2)}) copy-start(f32[5120]{0:T(1024)} %param.7) | copy-start | bytes 61444
  7.2 59.8 %all-gather.2.cloned.1.call-start = ((), (), s32[]{:S(2)}) async-start(), calls=%async_computation.6 | async-start | bytes 5570560 | tf_op jit(solution)/shard_map/all_gather | solution.py:39
  25.0 10.5 %all-to-all-start.1 = ((f32[16,1,1]{2,1,0:T(1,128)}), f32[16,1,1]{2,1,0:T(1,128)S(1)}, u32[]{:S(2)}, u32[]{:S(2)}) async-start(f32[16,1,1]{2,1,0:T(1,128)} %broadcast_in_dim.34), calls=%async_computation.1 | async-start | bytes 16384 | tf_op jit(solution)/shard_map/all_to_all | solution.py:16
  29.1 114.6 %reduce-scatter.2.cloned.1.call-start = ((), (), s32[]{:S(2)}) async-start(), calls=%async_computation.7 | async-start | bytes 11141120 | tf_op jit(solution)/shard_map/reduce_scatter | solution.py:49
  39.5 3.2 %copy-start.1 = (bf16[1,1,128,512]{3,2,1,0:T(8,128)(2,1)S(1)}, bf16[1,1,128,512]{3,2,1,0:T(8,128)(2,1)}, u32[]{:S(2)}) copy-start(bf16[1,1,128,512]{3,2,1,0:T(8,128)(2,1)} %param.9) | copy-start | bytes 393220
  82.0 63.8 %all-to-all-start.4 = ((f32[16,1,20]{2,1,0:T(1,128)}), f32[16,1,20]{2,1,0:T(1,128)S(1)}, u32[]{:S(2)}, u32[]{:S(2)}) async-start(f32[16,1,20]{2,1,0:T(1,128)} %all_to_all.27), calls=%async_computation.5 | async-start | bytes 16384 | tf_op jit(solution)/shard_map/all_to_all | solution.py:56
  145.8 18.8 %all-to-all-start.2 = ((f32[16,20,512]{2,1,0:T(8,128)}), f32[16,20,512]{2,1,0:T(8,128)S(1)}, u32[]{:S(2)}, u32[]{:S(2)}) async-start(f32[16,20,512]{2,1,0:T(8,128)} %reshape.95), calls=%async_computation.3 | async-start | bytes 1572864 | tf_op jit(solution)/shard_map/all_to_all | solution.py:53
Sparse Core Ops, SparseCore 0:
  23.9 43.0 all-gather.1
  69.5 74.2 reduce-scatter.1

commit v6 on v5

--- a/solution.py
+++ b/solution.py
@@ -47,9 +47,12 @@
         normed, scaled_cot, (((0,), (0,)), ((), ())), preferred_element_type=jnp.float32
     )
     grad_part = lax.psum_scatter(
-        grad_part.reshape(n_dp, features // n_dp, kv_width), "dp", scatter_dimension=0, tiled=True
+        grad_part.reshape(n_dp, features // n_dp, kv_width).astype(jnp.bfloat16),
+        "dp",
+        scatter_dimension=0,
+        tiled=True,
     )
-    grad_part = grad_part.reshape(n_group, shard_rows, kv_width)
+    grad_part = grad_part.astype(jnp.float32).reshape(n_group, shard_rows, kv_width)
     weight_grad = lax.all_to_all(grad_part, "group", 0, 0, tiled=True).sum(0)
     gain_part = lax.all_to_all(gain_term.reshape(n_dp, features // n_dp), "dp", 0, 0, tiled=True)
     gain_part = gain_part.sum(0).reshape(n_group, shard_rows)

time: 173 us -> 163 us (0.942)
  waiting for transfers between devices: 87.3 us -> 78.3 us
    reduce_scatter x1, waiting for transfers between devices: 55.3 us -> 45.4 us  [body(): lax.psum_scatter(grad_part.reshape(n_dp, features // n_dp, kv_width).asty...]
where the time goes in v6:
time: 163 us; the launch traced here: 162 us
  waiting for transfers between devices  78.3 us (48%)
  blocking collectives  24.7 us (15%)
  between operations  18.1 us (11%)
  starting transfers between devices  17.4 us (11%)
  matrix products  13.7 us (8%)
  local copies, waits for them, and re-layouts  6.51 us (4%)
  other arithmetic  3.2 us (2%)
    reduce_scatter x1, waiting for transfers between devices, body(): lax.psum_scatter(grad_part.reshape(n_dp, features // n_dp, kv_width).asty...  45.4 us
    all_gather x1, waiting for transfers between devices, body(): full_weight = lax.all_gather(part, 'dp', axis=0, tiled=True)  20.3 us
    all_to_all x1, blocking collectives, body(): lax.all_to_all(jnp.broadcast_to(value_weight[None], (n_group,) + value_we...  14.8 us
    all_to_all x1, blocking collectives, body(): lax.all_to_all(gain_term.reshape(n_dp, features // n_dp), 'dp', 0, 0, til...  9.9 us
    all_to_all x1, waiting for transfers between devices, body(): weight_grad = lax.all_to_all(grad_part, 'group', 0, 0, tiled=True).sum(0)  7.35 us
    all_to_all x1, starting transfers between devices, body(): weight_grad = lax.all_to_all(grad_part, 'group', 0, 0, tiled=True).sum(0)  6.7 us
    all_to_all x1, starting transfers between devices, body(): gain_grad = lax.all_to_all(gain_part, 'group', 0, 0, tiled=True).sum(0)  6.47 us
    all_to_all x1, waiting for transfers between devices, body(): lax.all_to_all(jnp.broadcast_to(scores.reshape(1, -1), (n_group, scores.s...  5.32 us
  transfers between devices with their start and end apart: 5, of which 4 were waited for; matrix products, arithmetic and copies ran while one was open for 13% of the time, Pallas kernels for 0%

profile of v6, /device:TPU:97, one launch (start us, length us, event | category | flops | bytes accessed | tf_op | source)
XLA Modules:
  0.0 161.9 jit_solution(6888291572416146831)
XLA Ops:
  7.2 0.0 copy-start
  7.2 0.0 copy-start.2
  7.2 0.0 all-gather.2.cloned.1.call-start
  7.2 0.9 broadcast_in_dim.32
  8.1 14.8 %all_to_all.34 = bf16[16,20,512]{2,1,0:T(8,128)(2,1)S(1)} all-to-all(bf16[16,20,512]{2,1,0:T(8,128)(2,1)S(1)} %broadcast_in_dim.32), channel_id=1, replica_groups=mesh['dp'=16,'group'=16] {'group'}, dimensions={0} | all-to-all | bytes 655360 | tf_op jit(solution)/shard_map/all_to_all | solution.py:36
  22.9 0.8 reshape.96
  23.7 0.0 all-gather.2.cloned.1.call-update
  24.4 0.6 broadcast_in_dim.34
  25.0 4.1 %all-to-all-start.1 = ((f32[16,1,1]{2,1,0:T(1,128)}), f32[16,1,1]{2,1,0:T(1,128)S(1)}, u32[]{:S(2)}, u32[]{:S(2)}) async-start(f32[16,1,1]{2,1,0:T(1,128)} %broadcast_in_dim.34), calls=%async_computation.1 | async-start | bytes 16384 | tf_op jit(solution)/shard_map/all_to_all | solution.py:16
  29.1 0.0 reduce-scatter.2.cloned.1.call-start
  29.8 0.0 copy-done
  29.8 0.3 fusion.2
  30.2 5.3 %all-to-all-done.1 = f32[16,1,1]{2,1,0:T(1,128)S(1)} async-done(((f32[16,1,1]{2,1,0:T(1,128)}), f32[16,1,1]{2,1,0:T(1,128)S(1)}, u32[]{:S(2)}, u32[]{:S(2)}) %all-to-all-start.1) | async-done | bytes 96 | tf_op jit(solution)/shard_map/all_to_all | solution.py:16
  35.5 0.6 reduce_sum.64
  38.1 0.1 copy.18
  38.1 0.6 multiply_reduce_fusion
  39.5 0.0 copy-done.2
  39.5 0.0 copy-start.1
  39.5 0.4 fusion.5
  39.9 1.4 copy.17
  41.4 0.0 copy-done.1
  41.4 5.3 %convolution_convert_fusion = bf16[16,320,512]{2,1,0:T(8,128)(2,1)} fusion(bf16[16,320,128]{2,1,0:T(8,128)(2,1)} %bitcast.35, bf16[1,1,128,512]{3,2,1,0:T(8,128)(2,1)S(1)} %copy-done.1, f32[128]{0:T(128)S(1)} %get-tuple-element.3), kind=kOutput, calls=%fused_computation.4 | convolution fusion | flops 673906688 | bytes 6685184 | tf_op jit(solution)/shard_map/dot_general | solution.py:46
  46.6 0.0 reduce-scatter.2.cloned.1.call-update
  46.7 20.3 %all-gather.2.cloned.1.call-done = bf16[5120,512]{1,0:T(8,128)(2,1)} async-done(((bf16[320,512]{1,0:T(8,128)(2,1)}), bf16[5120,512]{1,0:T(8,128)(2,1)}) %all-gather.2.cloned.1.call-update) | async-done | bytes 5242896 | tf_op jit(solution)/shard_map/all_gather | solution.py:39
  67.0 4.3 %fusion.3 = f32[5120]{0:T(1024)S(1)} fusion(bf16[5120,512]{1,0:T(8,128)(2,1)} %all-gather.2.cloned.1.call-done, bf16[1,1,128,5120]{3,2,1,0:T(8,128)(2,1)S(1)} %copy-done, f32[128]{0:T(128)S(1)} %get-tuple-element.4, bf16[1,1,128,512]{3,2,1,0:T(8,128)(2,1)S(1)} %copy-done.1, f32[128]{0:T(128)S(1)} %get-tuple-element.3), kind=kOutput, calls=%fused_computation.7 | convolution fusion | flops 673901568 | bytes 6706176 | tf_op jit(solution)/shard_map/dot_general | solution.py:41
  71.3 0.1 all_to_all.25
  71.4 9.9 %all_to_all.35 = f32[16,1,320]{2,1,0:T(1,128)S(1)} all-to-all(f32[16,1,320]{2,1,0:T(1,128)S(1)} %all_to_all.25), channel_id=1, replica_groups=mesh['dp'=16,'group'=16] {'dp'}, dimensions={0} | all-to-all | bytes 40960 | tf_op jit(solution)/shard_map/all_to_all | solution.py:57
  81.3 0.7 all_to_all.27
  82.0 6.5 %all-to-all-start.4 = ((f32[16,1,20]{2,1,0:T(1,128)}), f32[16,1,20]{2,1,0:T(1,128)S(1)}, u32[]{:S(2)}, u32[]{:S(2)}) async-start(f32[16,1,20]{2,1,0:T(1,128)} %all_to_all.27), calls=%async_computation.5 | async-start | bytes 16384 | tf_op jit(solution)/shard_map/all_to_all | solution.py:59
  88.5 45.4 %reduce-scatter.2.cloned.1.call-done = bf16[1,320,512]{2,1,0:T(8,128)(2,1)} async-done(((bf16[16,320,512]{2,1,0:T(8,128)(2,1)}), bf16[1,320,512]{2,1,0:T(8,128)(2,1)}) %reduce-scatter.2.cloned.1.call-update) | async-done | bytes 327696 | tf_op jit(solution)/shard_map/reduce_scatter | solution.py:49
  133.8 1.9 %reshape.104 = f32[16,20,512]{2,1,0:T(8,128)} reshape(bf16[1,320,512]{2,1,0:T(8,128)(2,1)} %reduce-scatter.2.cloned.1.call-done) | data formatting | bytes 983040 | tf_op jit(solution)/shard_map/reshape | solution.py:55
  135.8 0.0 all-to-all-done.4
  135.8 6.7 %all-to-all-start.2 = ((f32[16,20,512]{2,1,0:T(8,128)}), f32[16,20,512]{2,1,0:T(8,128)S(1)}, u32[]{:S(2)}, u32[]{:S(2)}) async-start(f32[16,20,512]{2,1,0:T(8,128)} %reshape.104), calls=%async_computation.3 | async-start | bytes 1572864 | tf_op jit(solution)/shard_map/all_to_all | solution.py:56
  142.5 4.0 %fusion.4 = bf16[1,1,128,512]{3,2,1,0:T(8,128)(2,1)} fusion(bf16[5120,512]{1,0:T(8,128)(2,1)} %all-gather.2.cloned.1.call-done, bf16[1,1,128,5120]{3,2,1,0:T(8,128)(2,1)S(1)} %copy-done, f32[5120]{0:T(1024)S(1)} %copy-done.2, f32[128]{0:T(128)S(1)} %get-tuple-element.4), kind=kOutput, calls=%fused_computation.9 | convolution fusion | flops 673775616 | bytes 6705664 | tf_op jit(solution)/shard_map/dot_general | solution.py:40
  146.5 0.5 reduce_sum.69
  147.1 7.3 %all-to-all-done.2 = f32[16,20,512]{2,1,0:T(8,128)S(1)} async-done(((f32[16,20,512]{2,1,0:T(8,128)}), f32[16,20,512]{2,1,0:T(8,128)S(1)}, u32[]{:S(2)}, u32[]{:S(2)}) %all-to-all-start.2) | async-done | bytes 655392 | tf_op jit(solution)/shard_map/all_to_all | solution.py:56
  154.4 0.7 reduce_sum.66
  (2 shorter events, 0.0 us)
Async XLA Ops:
  7.2 22.7 %copy-start = (bf16[1,1,128,5120]{3,2,1,0:T(8,128)(2,1)S(1)}, bf16[1,1,128,5120]{3,2,1,0:T(8,128)(2,1)}, u32[]{:S(2)}) copy-start(bf16[1,1,128,5120]{3,2,1,0:T(8,128)(2,1)} %param.6) | copy-start | bytes 3932164
  7.2 32.3 %copy-start.2 = (f32[5120]{0:T(1024)S(1)}, f32[5120]{0:T(1024)}, u32[]{:S(2)}) copy-start(f32[5120]{0:T(1024)} %param.7) | copy-start | bytes 61444
  7.2 59.8 %all-gather.2.cloned.1.call-start = ((), (), s32[]{:S(2)}) async-start(), calls=%async_computation.6 | async-start | bytes 5570560 | tf_op jit(solution)/shard_map/all_gather | solution.py:39
  25.0 10.5 %all-to-all-start.1 = ((f32[16,1,1]{2,1,0:T(1,128)}), f32[16,1,1]{2,1,0:T(1,128)S(1)}, u32[]{:S(2)}, u32[]{:S(2)}) async-start(f32[16,1,1]{2,1,0:T(1,128)} %broadcast_in_dim.34), calls=%async_computation.1 | async-start | bytes 16384 | tf_op jit(solution)/shard_map/all_to_all | solution.py:16
  29.1 104.7 %reduce-scatter.2.cloned.1.call-start = ((), (), s32[]{:S(2)}) async-start(), calls=%async_computation.7 | async-start | bytes 5570560 | tf_op jit(solution)/shard_map/reduce_scatter | solution.py:49
  39.5 1.8 %copy-start.1 = (bf16[1,1,128,512]{3,2,1,0:T(8,128)(2,1)S(1)}, bf16[1,1,128,512]{3,2,1,0:T(8,128)(2,1)}, u32[]{:S(2)}) copy-start(bf16[1,1,128,512]{3,2,1,0:T(8,128)(2,1)} %param.9) | copy-start | bytes 393220
  82.0 53.8 %all-to-all-start.4 = ((f32[16,1,20]{2,1,0:T(1,128)}), f32[16,1,20]{2,1,0:T(1,128)S(1)}, u32[]{:S(2)}, u32[]{:S(2)}) async-start(f32[16,1,20]{2,1,0:T(1,128)} %all_to_all.27), calls=%async_computation.5 | async-start | bytes 16384 | tf_op jit(solution)/shard_map/all_to_all | solution.py:59
  135.8 18.6 %all-to-all-start.2 = ((f32[16,20,512]{2,1,0:T(8,128)}), f32[16,20,512]{2,1,0:T(8,128)S(1)}, u32[]{:S(2)}, u32[]{:S(2)}) async-start(f32[16,20,512]{2,1,0:T(8,128)} %reshape.104), calls=%async_computation.3 | async-start | bytes 1572864 | tf_op jit(solution)/shard_map/all_to_all | solution.py:56
Sparse Core Ops, SparseCore 0:
  23.9 43.0 all-gather.1
  69.5 64.2 reduce-scatter.1

commit v7 on v5

--- a/solution.py
+++ b/solution.py
@@ -43,14 +43,18 @@
     )
     gain_term = jnp.sum(back * (flat_in.astype(jnp.float32) * inverse), axis=0)
     values = projected.astype(jnp.bfloat16).reshape(prompts, answers, length, kv_width)
-    grad_part = lax.dot_general(
-        normed, scaled_cot, (((0,), (0,)), ((), ())), preferred_element_type=jnp.float32
-    )
-    grad_part = lax.psum_scatter(
-        grad_part.reshape(n_dp, features // n_dp, kv_width), "dp", scatter_dimension=0, tiled=True
-    )
-    grad_part = grad_part.reshape(n_group, shard_rows, kv_width)
-    weight_grad = lax.all_to_all(grad_part, "group", 0, 0, tiled=True).sum(0)
+    half = kv_width // 2
+    grad_halves = []
+    for lo in (0, half):
+        grad_part = lax.dot_general(
+            normed, scaled_cot[:, lo:lo + half], (((0,), (0,)), ((), ())), preferred_element_type=jnp.float32
+        )
+        grad_part = lax.psum_scatter(
+            grad_part.reshape(n_dp, features // n_dp, half), "dp", scatter_dimension=0, tiled=True
+        )
+        grad_part = grad_part.reshape(n_group, shard_rows, half)
+        grad_halves.append(lax.all_to_all(grad_part, "group", 0, 0, tiled=True).sum(0))
+    weight_grad = jnp.concatenate(grad_halves, axis=1)
     gain_part = lax.all_to_all(gain_term.reshape(n_dp, features // n_dp), "dp", 0, 0, tiled=True)
     gain_part = gain_part.sum(0).reshape(n_group, shard_rows)
     gain_grad = lax.all_to_all(gain_part, "group", 0, 0, tiled=True).sum(0)

time: 173 us -> 226 us (1.31)
  waiting for transfers between devices: 87.3 us -> 130 us
  starting transfers between devices: 16.8 us -> 23.8 us
    reduce_scatter x1 -> x2, waiting for transfers between devices: 55.3 us -> 104 us  [body(): lax.psum_scatter(grad_part.reshape(n_dp, features // n_dp, half), 'dp', s...]
    all_to_all x1 -> x2, starting transfers between devices: 6.14 us -> 13.2 us  [body(): lax.all_to_all(grad_part, 'group', 0, 0, tiled=True).sum(0)]
    all_to_all x1 -> x2, waiting for transfers between devices: 8.05 us -> 3.38 us  [body(): lax.all_to_all(grad_part, 'group', 0, 0, tiled=True).sum(0)]
    all_to_all x1, waiting for transfers between devices: 5.32 us -> 1.99 us  [body(): lax.all_to_all(jnp.broadcast_to(scores.reshape(1, -1), (n_group, scores.s...]
    all_gather x1, waiting for transfers between devices: 18.6 us -> 20.9 us  [body(): full_weight = lax.all_gather(part, 'dp', axis=0, tiled=True)]
    dot_general x1 -> x2, matrix products: 5.57 us -> 6.38 us  [body(): lax.dot_general(normed, scaled_cot[:, lo:lo + half], (((0,), (0,)), ((),...]
  transfers between devices with their start and end apart: 5 -> 7, of which waited for: 4 -> 5; matrix products, arithmetic and copies ran while one was open for 13% -> 11% of each run, Pallas kernels for 0% -> 0%
where the time goes in v7:
time: 226 us; the launch traced here: 224 us
  waiting for transfers between devices  130 us (58%)
  blocking collectives  24.7 us (11%)
  starting transfers between devices  23.8 us (11%)
  between operations  17.9 us (8%)
  matrix products  14.7 us (7%)
  local copies, waits for them, and re-layouts  8.46 us (4%)
  other arithmetic  4.4 us (2%)
    reduce_scatter x2, waiting for transfers between devices, body(): lax.psum_scatter(grad_part.reshape(n_dp, features // n_dp, half), 'dp', s...  104 us
    all_gather x1, waiting for transfers between devices, body(): full_weight = lax.all_gather(part, 'dp', axis=0, tiled=True)  20.9 us
    all_to_all x1, blocking collectives, body(): lax.all_to_all(jnp.broadcast_to(value_weight[None], (n_group,) + value_we...  14.8 us
    all_to_all x2, starting transfers between devices, body(): lax.all_to_all(grad_part, 'group', 0, 0, tiled=True).sum(0)  13.2 us
    all_to_all x1, blocking collectives, body(): lax.all_to_all(gain_term.reshape(n_dp, features // n_dp), 'dp', 0, 0, til...  9.86 us
    all_to_all x1, starting transfers between devices, body(): gain_grad = lax.all_to_all(gain_part, 'group', 0, 0, tiled=True).sum(0)  6.41 us
    dot_general x2, matrix products, body(): lax.dot_general(normed, scaled_cot[:, lo:lo + half], (((0,), (0,)), ((),...  6.38 us
  transfers between devices with their start and end apart: 7, of which 5 were waited for; matrix products, arithmetic and copies ran while one was open for 11% of the time, Pallas kernels for 0%

profile of v7, /device:TPU:97, one launch (start us, length us, event | category | flops | bytes accessed | tf_op | source)
XLA Modules:
  0.0 223.9 jit_solution(13681017191442583488)
XLA Ops:
  7.2 0.0 copy-start
  7.2 0.0 copy-start.2
  7.2 0.0 all-gather.2.cloned.1.call-start
  7.2 0.9 broadcast_in_dim.32
  8.1 14.8 %all_to_all.39 = bf16[16,20,512]{2,1,0:T(8,128)(2,1)S(1)} all-to-all(bf16[16,20,512]{2,1,0:T(8,128)(2,1)S(1)} %broadcast_in_dim.32), channel_id=1, replica_groups=mesh['dp'=16,'group'=16] {'group'}, dimensions={0} | all-to-all | bytes 655360 | tf_op jit(solution)/shard_map/all_to_all | solution.py:36
  22.9 0.8 reshape.90
  23.7 0.0 all-gather.2.cloned.1.call-update
  24.4 0.6 broadcast_in_dim.34
  25.0 4.1 %all-to-all-start.1 = ((f32[16,1,1]{2,1,0:T(1,128)}), f32[16,1,1]{2,1,0:T(1,128)S(1)}, u32[]{:S(2)}, u32[]{:S(2)}) async-start(f32[16,1,1]{2,1,0:T(1,128)} %broadcast_in_dim.34), calls=%async_computation.1 | async-start | bytes 16384 | tf_op jit(solution)/shard_map/all_to_all | solution.py:16
  29.1 0.0 reduce-scatter.3.cloned.1.call-start
  29.8 0.0 copy-done
  29.8 0.3 fusion.2
  30.2 0.0 copy-done.2
  30.2 0.0 copy-start.1
  30.2 1.5 fusion.5
  31.7 1.8 copy.18
  33.5 2.0 all-to-all-done.1
  35.5 0.6 reduce_sum.73
  38.0 0.1 copy.19
  38.1 0.6 multiply_reduce_fusion
  39.5 0.0 copy-done.1
  39.5 0.1 fusion.7
  39.6 3.2 %fusion.9 = f32[16,320,256]{2,1,0:T(8,128)} fusion(bf16[16,320,128]{2,1,0:T(8,128)(2,1)S(1)} %bitcast.34, bf16[128,512]{1,0:T(8,128)(2,1)S(1)} %fusion.7), kind=kOutput, calls=%fused_computation.15 | convolution fusion | flops 335544320 | bytes 6619136 | tf_op jit(solution)/shard_map/dot_general | solution.py:49
  42.8 0.0 reduce-scatter.3.cloned.1.call-update
  42.8 0.0 reduce-scatter.5.cloned.1.call-start
  42.9 3.2 %fusion.8 = f32[16,320,256]{2,1,0:T(8,128)} fusion(bf16[16,320,128]{2,1,0:T(8,128)(2,1)S(1)} %bitcast.35, bf16[128,512]{1,0:T(8,128)(2,1)S(1)} %fusion.7), kind=kOutput, calls=%fused_computation.13 | convolution fusion | flops 335544320 | bytes 6619136 | tf_op jit(solution)/shard_map/dot_general | solution.py:49
  46.0 0.0 reduce-scatter.5.cloned.1.call-update
  46.1 20.9 %all-gather.2.cloned.1.call-done = bf16[5120,512]{1,0:T(8,128)(2,1)} async-done(((bf16[320,512]{1,0:T(8,128)(2,1)}), bf16[5120,512]{1,0:T(8,128)(2,1)}) %all-gather.2.cloned.1.call-update) | async-done | bytes 5242896 | tf_op jit(solution)/shard_map/all_gather | solution.py:39
  67.0 4.3 %fusion.3 = f32[5120]{0:T(1024)S(1)} fusion(bf16[128,512]{1,0:T(8,128)(2,1)S(1)} %fusion.7, bf16[5120,512]{1,0:T(8,128)(2,1)} %all-gather.2.cloned.1.call-done, bf16[1,1,128,5120]{3,2,1,0:T(8,128)(2,1)S(1)} %copy-done, f32[128]{0:T(128)S(1)} %add_rsqrt_fusion), kind=kOutput, calls=%fused_computation.6 | convolution fusion | flops 673704960 | bytes 6705664 | tf_op jit(solution)/shard_map/dot_general | solution.py:41
  71.3 0.1 all_to_all.29
  71.4 9.9 %all_to_all.40 = f32[16,1,320]{2,1,0:T(1,128)S(1)} all-to-all(f32[16,1,320]{2,1,0:T(1,128)S(1)} %all_to_all.29), channel_id=1, replica_groups=mesh['dp'=16,'group'=16] {'dp'}, dimensions={0} | all-to-all | bytes 40960 | tf_op jit(solution)/shard_map/all_to_all | solution.py:58
  81.3 0.7 all_to_all.31
  82.0 6.4 %all-to-all-start.5 = ((f32[16,1,20]{2,1,0:T(1,128)}), f32[16,1,20]{2,1,0:T(1,128)S(1)}, u32[]{:S(2)}, u32[]{:S(2)}) async-start(f32[16,1,20]{2,1,0:T(1,128)} %all_to_all.31), calls=%async_computation.7 | async-start | bytes 16384 | tf_op jit(solution)/shard_map/all_to_all | solution.py:60
  88.4 45.5 %reduce-scatter.3.cloned.1.call-done = f32[1,320,256]{2,1,0:T(8,128)} async-done(((f32[16,320,256]{2,1,0:T(8,128)}), f32[1,320,256]{2,1,0:T(8,128)}) %reduce-scatter.3.cloned.1.call-update) | async-done | bytes 327696 | tf_op jit(solution)/shard_map/reduce_scatter | solution.py:52
  133.9 1.8 reshape.92
  135.7 0.0 all-to-all-done.5
  135.7 6.7 %all-to-all-start.2 = ((f32[16,20,256]{2,1,0:T(8,128)}), f32[16,20,256]{2,1,0:T(8,128)S(1)}, u32[]{:S(2)}, u32[]{:S(2)}) async-start(f32[16,20,256]{2,1,0:T(8,128)} %reshape.92), calls=%async_computation.3 | async-start | bytes 786432 | tf_op jit(solution)/shard_map/all_to_all | solution.py:56
  142.4 58.1 %reduce-scatter.5.cloned.1.call-done = f32[1,320,256]{2,1,0:T(8,128)} async-done(((f32[16,320,256]{2,1,0:T(8,128)}), f32[1,320,256]{2,1,0:T(8,128)}) %reduce-scatter.5.cloned.1.call-update) | async-done | bytes 327696 | tf_op jit(solution)/shard_map/reduce_scatter | solution.py:52
  200.5 1.7 reshape.93
  202.3 0.0 all-to-all-done.2
  202.3 6.5 %all-to-all-start.3 = ((f32[16,20,256]{2,1,0:T(8,128)}), f32[16,20,256]{2,1,0:T(8,128)S(1)}, u32[]{:S(2)}, u32[]{:S(2)}) async-start(f32[16,20,256]{2,1,0:T(8,128)} %reshape.93), calls=%async_computation.5 | async-start | bytes 786432 | tf_op jit(solution)/shard_map/all_to_all | solution.py:56
  208.7 4.0 %fusion.4 = bf16[1,1,128,512]{3,2,1,0:T(8,128)(2,1)} fusion(bf16[5120,512]{1,0:T(8,128)(2,1)} %all-gather.2.cloned.1.call-done, bf16[1,1,128,5120]{3,2,1,0:T(8,128)(2,1)S(1)} %copy-done, f32[5120]{0:T(1024)S(1)} %copy-done.2, f32[128]{0:T(128)S(1)} %add_rsqrt_fusion), kind=kOutput, calls=%fused_computation.8 | convolution fusion | flops 673775616 | bytes 6705664 | tf_op jit(solution)/shard_map/dot_general | solution.py:40
  212.8 0.5 reduce_sum.79
  213.4 3.4 %all-to-all-done.3 = f32[16,20,256]{2,1,0:T(8,128)S(1)} async-done(((f32[16,20,256]{2,1,0:T(8,128)}), f32[16,20,256]{2,1,0:T(8,128)S(1)}, u32[]{:S(2)}, u32[]{:S(2)}) %all-to-all-start.3) | async-done | bytes 327712 | tf_op jit(solution)/shard_map/all_to_all | solution.py:56
  216.8 0.6 pad_maximum_fusion
  (5 shorter events, 0.1 us)
Async XLA Ops:
  7.2 22.7 %copy-start = (bf16[1,1,128,5120]{3,2,1,0:T(8,128)(2,1)S(1)}, bf16[1,1,128,5120]{3,2,1,0:T(8,128)(2,1)}, u32[]{:S(2)}) copy-start(bf16[1,1,128,5120]{3,2,1,0:T(8,128)(2,1)} %param.6) | copy-start | bytes 3932164
  7.2 23.0 %copy-start.2 = (f32[5120]{0:T(1024)S(1)}, f32[5120]{0:T(1024)}, u32[]{:S(2)}) copy-start(f32[5120]{0:T(1024)} %param.7) | copy-start | bytes 61444
  7.2 59.8 %all-gather.2.cloned.1.call-start = ((), (), s32[]{:S(2)}) async-start(), calls=%async_computation.8 | async-start | bytes 5570560 | tf_op jit(solution)/shard_map/all_gather | solution.py:39
  25.0 10.5 %all-to-all-start.1 = ((f32[16,1,1]{2,1,0:T(1,128)}), f32[16,1,1]{2,1,0:T(1,128)S(1)}, u32[]{:S(2)}, u32[]{:S(2)}) async-start(f32[16,1,1]{2,1,0:T(1,128)} %broadcast_in_dim.34), calls=%async_computation.1 | async-start | bytes 16384 | tf_op jit(solution)/shard_map/all_to_all | solution.py:16
  29.1 104.8 %reduce-scatter.3.cloned.1.call-start = ((), (), s32[]{:S(2)}) async-start(), calls=%async_computation.9 | async-start | bytes 5570560 | tf_op jit(solution)/shard_map/reduce_scatter | solution.py:52
  30.2 9.3 %copy-start.1 = (bf16[1,1,128,512]{3,2,1,0:T(8,128)(2,1)S(1)}, bf16[1,1,128,512]{3,2,1,0:T(8,128)(2,1)}, u32[]{:S(2)}) copy-start(bf16[1,1,128,512]{3,2,1,0:T(8,128)(2,1)} %param.9) | copy-start | bytes 393220
  42.8 157.7 %reduce-scatter.5.cloned.1.call-start = ((), (), s32[]{:S(2)}) async-start(), calls=%async_computation.10 | async-start | bytes 5570560 | tf_op jit(solution)/shard_map/reduce_scatter | solution.py:52
  82.0 53.7 %all-to-all-start.5 = ((f32[16,1,20]{2,1,0:T(1,128)}), f32[16,1,20]{2,1,0:T(1,128)S(1)}, u32[]{:S(2)}, u32[]{:S(2)}) async-start(f32[16,1,20]{2,1,0:T(1,128)} %all_to_all.31), calls=%async_computation.7 | async-start | bytes 16384 | tf_op jit(solution)/shard_map/all_to_all | solution.py:60
  135.7 66.6 %all-to-all-start.2 = ((f32[16,20,256]{2,1,0:T(8,128)}), f32[16,20,256]{2,1,0:T(8,128)S(1)}, u32[]{:S(2)}, u32[]{:S(2)}) async-start(f32[16,20,256]{2,1,0:T(8,128)} %reshape.92), calls=%async_computation.3 | async-start | bytes 786432 | tf_op jit(solution)/shard_map/all_to_all | solution.py:56
  202.3 14.5 %all-to-all-start.3 = ((f32[16,20,256]{2,1,0:T(8,128)}), f32[16,20,256]{2,1,0:T(8,128)S(1)}, u32[]{:S(2)}, u32[]{:S(2)}) async-start(f32[16,20,256]{2,1,0:T(8,128)} %reshape.93), calls=%async_computation.5 | async-start | bytes 786432 | tf_op jit(solution)/shard_map/all_to_all | solution.py:56
Sparse Core Ops, SparseCore 0:
  23.9 43.0 all-gather.1
  69.5 64.3 reduce-scatter.2
  136.5 64.0 reduce-scatter.4

commit v8 on v5

--- a/solution.py
+++ b/solution.py
@@ -50,7 +50,8 @@
         grad_part.reshape(n_dp, features // n_dp, kv_width), "dp", scatter_dimension=0, tiled=True
     )
     grad_part = grad_part.reshape(n_group, shard_rows, kv_width)
-    weight_grad = lax.all_to_all(grad_part, "group", 0, 0, tiled=True).sum(0)
+    weight_grad = lax.all_to_all(grad_part.astype(jnp.bfloat16), "group", 0, 0, tiled=True)
+    weight_grad = weight_grad.astype(jnp.float32).sum(0)
     gain_part = lax.all_to_all(gain_term.reshape(n_dp, features // n_dp), "dp", 0, 0, tiled=True)
     gain_part = gain_part.sum(0).reshape(n_group, shard_rows)
     gain_grad = lax.all_to_all(gain_part, "group", 0, 0, tiled=True).sum(0)

time: 173 us -> 169 us (0.977)
  waiting for transfers between devices: 87.3 us -> 82.8 us
    all_to_all x1, waiting for transfers between devices: 8.05 us -> 3.57 us  [body(): lax.all_to_all(grad_part.astype(jnp.bfloat16), 'group', 0, 0, tiled=True)]
    reshape x1 -> x0, local copies, waits for them, and re-layouts: 2.03 us -> none  [body(): grad_part = grad_part.reshape(n_group, shard_rows, kv_width)]
where the time goes in v8:
time: 169 us; the launch traced here: 168 us
  waiting for transfers between devices  82.8 us (49%)
  blocking collectives  24.7 us (15%)
  between operations  18.1 us (11%)
  starting transfers between devices  16.8 us (10%)
  matrix products  13.9 us (8%)
  local copies, waits for them, and re-layouts  5.7 us (3%)
  other arithmetic  5.4 us (3%)
    reduce_scatter x1, waiting for transfers between devices, body(): lax.psum_scatter(grad_part.reshape(n_dp, features // n_dp, kv_width), 'dp...  55.3 us
    all_gather x1, waiting for transfers between devices, body(): full_weight = lax.all_gather(part, 'dp', axis=0, tiled=True)  18.6 us
    all_to_all x1, blocking collectives, body(): lax.all_to_all(jnp.broadcast_to(value_weight[None], (n_group,) + value_we...  14.8 us
    all_to_all x1, blocking collectives, body(): lax.all_to_all(gain_term.reshape(n_dp, features // n_dp), 'dp', 0, 0, til...  9.89 us
    all_to_all x1, starting transfers between devices, body(): gain_grad = lax.all_to_all(gain_part, 'group', 0, 0, tiled=True).sum(0)  6.47 us
    all_to_all x1, starting transfers between devices, body(): lax.all_to_all(grad_part.astype(jnp.bfloat16), 'group', 0, 0, tiled=True)  6.14 us
    dot_general x1, matrix products, body(): lax.dot_general(normed, scaled_cot, (((0,), (0,)), ((), ())), preferred_e...  5.57 us
    all_to_all x1, waiting for transfers between devices, body(): lax.all_to_all(jnp.broadcast_to(scores.reshape(1, -1), (n_group, scores.s...  5.32 us
  transfers between devices with their start and end apart: 5, of which 4 were waited for; matrix products, arithmetic and copies ran while one was open for 13% of the time, Pallas kernels for 0%

profile of v8, /device:TPU:97, one launch (start us, length us, event | category | flops | bytes accessed | tf_op | source)
XLA Modules:
  0.0 167.5 jit_solution(5549544853270615096)
XLA Ops:
  7.2 0.0 copy-start
  7.2 0.0 copy-start.2
  7.2 0.0 all-gather.2.cloned.1.call-start
  7.2 0.9 broadcast_in_dim.32
  8.1 14.8 %all_to_all.34 = bf16[16,20,512]{2,1,0:T(8,128)(2,1)S(1)} all-to-all(bf16[16,20,512]{2,1,0:T(8,128)(2,1)S(1)} %broadcast_in_dim.32), channel_id=1, replica_groups=mesh['dp'=16,'group'=16] {'group'}, dimensions={0} | all-to-all | bytes 655360 | tf_op jit(solution)/shard_map/all_to_all | solution.py:36
  22.9 0.8 reshape.92
  23.7 0.0 all-gather.2.cloned.1.call-update
  24.4 0.6 broadcast_in_dim.34
  25.0 4.1 %all-to-all-start.1 = ((f32[16,1,1]{2,1,0:T(1,128)}), f32[16,1,1]{2,1,0:T(1,128)S(1)}, u32[]{:S(2)}, u32[]{:S(2)}) async-start(f32[16,1,1]{2,1,0:T(1,128)} %broadcast_in_dim.34), calls=%async_computation.1 | async-start | bytes 16384 | tf_op jit(solution)/shard_map/all_to_all | solution.py:16
  29.1 0.0 reduce-scatter.2.cloned.1.call-start
  29.8 0.0 copy-done
  29.8 0.3 fusion.2
  30.2 5.3 %all-to-all-done.1 = f32[16,1,1]{2,1,0:T(1,128)S(1)} async-done(((f32[16,1,1]{2,1,0:T(1,128)}), f32[16,1,1]{2,1,0:T(1,128)S(1)}, u32[]{:S(2)}, u32[]{:S(2)}) %all-to-all-start.1) | async-done | bytes 96 | tf_op jit(solution)/shard_map/all_to_all | solution.py:16
  35.5 0.6 reduce_sum.64
  38.1 0.1 copy.18
  38.1 0.6 multiply_reduce_fusion
  39.5 0.0 copy-done.2
  39.5 0.0 copy-start.1
  39.5 1.5 fusion.5
  41.0 1.8 %copy.17 = bf16[5120,128]{1,0:T(8,128)(2,1)S(1)} copy(bf16[5120,128]{0,1:T(8,128)(2,1)} %fusion.5) | data formatting | bytes 2621440 | tf_op jit(solution)/shard_map/dot_general | solution.py:46
  42.7 0.0 copy-done.1
  42.8 5.6 %fusion.12 = f32[16,320,512]{2,1,0:T(8,128)} fusion(bf16[16,320,128]{2,1,0:T(8,128)(2,1)S(1)} %bitcast.35, bf16[1,1,128,512]{3,2,1,0:T(8,128)(2,1)S(1)} %copy-done.1, f32[128]{0:T(128)S(1)} %get-tuple-element.3), kind=kOutput, calls=%fused_computation.17 | convolution fusion | flops 671285248 | bytes 11928064 | tf_op jit(solution)/shard_map/dot_general | solution.py:46
  48.3 0.0 reduce-scatter.2.cloned.1.call-update
  48.4 18.6 %all-gather.2.cloned.1.call-done = bf16[5120,512]{1,0:T(8,128)(2,1)} async-done(((bf16[320,512]{1,0:T(8,128)(2,1)}), bf16[5120,512]{1,0:T(8,128)(2,1)}) %all-gather.2.cloned.1.call-update) | async-done | bytes 5242896 | tf_op jit(solution)/shard_map/all_gather | solution.py:39
  66.9 4.3 %fusion.3 = f32[5120]{0:T(1024)S(1)} fusion(bf16[5120,512]{1,0:T(8,128)(2,1)} %all-gather.2.cloned.1.call-done, bf16[1,1,128,5120]{3,2,1,0:T(8,128)(2,1)S(1)} %copy-done, f32[128]{0:T(128)S(1)} %get-tuple-element.4, bf16[1,1,128,512]{3,2,1,0:T(8,128)(2,1)S(1)} %copy-done.1, f32[128]{0:T(128)S(1)} %get-tuple-element.3), kind=kOutput, calls=%fused_computation.6 | convolution fusion | flops 673901568 | bytes 6706176 | tf_op jit(solution)/shard_map/dot_general | solution.py:41
  71.3 0.1 all_to_all.25
  71.4 9.9 %all_to_all.35 = f32[16,1,320]{2,1,0:T(1,128)S(1)} all-to-all(f32[16,1,320]{2,1,0:T(1,128)S(1)} %all_to_all.25), channel_id=1, replica_groups=mesh['dp'=16,'group'=16] {'dp'}, dimensions={0} | all-to-all | bytes 40960 | tf_op jit(solution)/shard_map/all_to_all | solution.py:55
  81.3 0.7 all_to_all.27
  82.0 6.5 %all-to-all-start.4 = ((f32[16,1,20]{2,1,0:T(1,128)}), f32[16,1,20]{2,1,0:T(1,128)S(1)}, u32[]{:S(2)}, u32[]{:S(2)}) async-start(f32[16,1,20]{2,1,0:T(1,128)} %all_to_all.27), calls=%async_computation.5 | async-start | bytes 16384 | tf_op jit(solution)/shard_map/all_to_all | solution.py:57
  88.5 55.3 %reduce-scatter.2.cloned.1.call-done = f32[1,320,512]{2,1,0:T(8,128)} async-done(((f32[16,320,512]{2,1,0:T(8,128)}), f32[1,320,512]{2,1,0:T(8,128)}) %reduce-scatter.2.cloned.1.call-update) | async-done | bytes 655376 | tf_op jit(solution)/shard_map/reduce_scatter | solution.py:49
  143.8 1.1 convert_element_type.55
  144.9 0.8 convert_element_type.56
  145.7 0.0 all-to-all-done.4
  145.7 6.1 %all-to-all-start.2 = ((bf16[16,20,512]{2,1,0:T(8,128)(2,1)}), bf16[16,20,512]{2,1,0:T(8,128)(2,1)S(1)}, u32[]{:S(2)}, u32[]{:S(2)}) async-start(bf16[16,20,512]{2,1,0:T(8,128)(2,1)} %convert_element_type.56), calls=%async_computation.3 | async-start | bytes 786432 | tf_op jit(solution)/shard_map/all_to_all | solution.py:53
  151.8 4.0 %fusion.4 = bf16[1,1,128,512]{3,2,1,0:T(8,128)(2,1)} fusion(bf16[5120,512]{1,0:T(8,128)(2,1)} %all-gather.2.cloned.1.call-done, bf16[1,1,128,5120]{3,2,1,0:T(8,128)(2,1)S(1)} %copy-done, f32[5120]{0:T(1024)S(1)} %copy-done.2, f32[128]{0:T(128)S(1)} %get-tuple-element.4), kind=kOutput, calls=%fused_computation.8 | convolution fusion | flops 673775616 | bytes 6705664 | tf_op jit(solution)/shard_map/dot_general | solution.py:40
  155.9 0.5 reduce_sum.69
  156.4 3.6 %all-to-all-done.2 = bf16[16,20,512]{2,1,0:T(8,128)(2,1)S(1)} async-done(((bf16[16,20,512]{2,1,0:T(8,128)(2,1)}), bf16[16,20,512]{2,1,0:T(8,128)(2,1)S(1)}, u32[]{:S(2)}, u32[]{:S(2)}) %all-to-all-start.2) | async-done | bytes 327712 | tf_op jit(solution)/shard_map/all_to_all | solution.py:53
  160.0 0.7 convert_reduce_fusion
  (2 shorter events, 0.0 us)
Async XLA Ops:
  7.2 22.7 %copy-start = (bf16[1,1,128,5120]{3,2,1,0:T(8,128)(2,1)S(1)}, bf16[1,1,128,5120]{3,2,1,0:T(8,128)(2,1)}, u32[]{:S(2)}) copy-start(bf16[1,1,128,5120]{3,2,1,0:T(8,128)(2,1)} %param.6) | copy-start | bytes 3932164
  7.2 32.3 %copy-start.2 = (f32[5120]{0:T(1024)S(1)}, f32[5120]{0:T(1024)}, u32[]{:S(2)}) copy-start(f32[5120]{0:T(1024)} %param.7) | copy-start | bytes 61444
  7.2 59.8 %all-gather.2.cloned.1.call-start = ((), (), s32[]{:S(2)}) async-start(), calls=%async_computation.6 | async-start | bytes 5570560 | tf_op jit(solution)/shard_map/all_gather | solution.py:39
  25.0 10.5 %all-to-all-start.1 = ((f32[16,1,1]{2,1,0:T(1,128)}), f32[16,1,1]{2,1,0:T(1,128)S(1)}, u32[]{:S(2)}, u32[]{:S(2)}) async-start(f32[16,1,1]{2,1,0:T(1,128)} %broadcast_in_dim.34), calls=%async_computation.1 | async-start | bytes 16384 | tf_op jit(solution)/shard_map/all_to_all | solution.py:16
  29.1 114.6 %reduce-scatter.2.cloned.1.call-start = ((), (), s32[]{:S(2)}) async-start(), calls=%async_computation.7 | async-start | bytes 11141120 | tf_op jit(solution)/shard_map/reduce_scatter | solution.py:49
  39.5 3.2 %copy-start.1 = (bf16[1,1,128,512]{3,2,1,0:T(8,128)(2,1)S(1)}, bf16[1,1,128,512]{3,2,1,0:T(8,128)(2,1)}, u32[]{:S(2)}) copy-start(bf16[1,1,128,512]{3,2,1,0:T(8,128)(2,1)} %param.9) | copy-start | bytes 393220
  82.0 63.7 %all-to-all-start.4 = ((f32[16,1,20]{2,1,0:T(1,128)}), f32[16,1,20]{2,1,0:T(1,128)S(1)}, u32[]{:S(2)}, u32[]{:S(2)}) async-start(f32[16,1,20]{2,1,0:T(1,128)} %all_to_all.27), calls=%async_computation.5 | async-start | bytes 16384 | tf_op jit(solution)/shard_map/all_to_all | solution.py:57
  145.7 14.3 %all-to-all-start.2 = ((bf16[16,20,512]{2,1,0:T(8,128)(2,1)}), bf16[16,20,512]{2,1,0:T(8,128)(2,1)S(1)}, u32[]{:S(2)}, u32[]{:S(2)}) async-start(bf16[16,20,512]{2,1,0:T(8,128)(2,1)} %convert_element_type.56), calls=%async_computation.3 | async-start | bytes 786432 | tf_op jit(solution)/shard_map/all_to_all | solution.py:53
Sparse Core Ops, SparseCore 0:
  23.9 43.0 all-gather.1
  69.5 74.2 reduce-scatter.1
